TPU v7x, 256 devices: a whole 4x4x8 slice. The times are simulated.
256 devices in a mesh: ctx: 64 (over z, y, core), head: 4 (over x).
Axes of the slice: x: 4, y: 4, z: 8, core: 2. Of those that a mesh axis runs over, the one named last changes fastest.
Arguments:
- delta_q: bfloat16 [16384, 2048], P('ctx', 'head'), may hold values from -6 to 6
- delta_k: bfloat16 [16384, 2048], P('ctx', 'head'), may hold values from -6 to 6
- delta_v: bfloat16 [16384, 2048], P('ctx', 'head'), may hold values from -6 to 6
- beta: float32 [16384, 16], P('ctx', 'head'), may hold values from 0 to 0.9, as said below
- log_decay: float32 [16384, 16], P('ctx', 'head'), may hold values from -1 to 0, as said below
- out_gate: bfloat16 [16384, 2048], P('ctx', 'head'), may hold values from -6 to 6
- norm_gain: float32 [128], replicated, may hold values from 0.1 to 1.9
- attn_q: bfloat16 [16384, 2048], P('ctx', 'head'), may hold values from -16 to 16
- attn_k: bfloat16 [16384, 2048], P('ctx', 'head'), may hold values from -16 to 16
- attn_v: bfloat16 [16384, 2048], P('ctx', 'head'), may hold values from -6 to 6
- w_delta_out: bfloat16 [2048, 2048], P('head'), may hold values from -0.125 to 0.125
- w_attn_out: bfloat16 [2048, 2048], P('head'), may hold values from -0.125 to 0.125
Outputs:
- branch_sum: bfloat16 [16384, 2048], P(('ctx', 'head'))
Inputs may be any that keep to these rules, and one draw needn't show every extreme that they name: `beta`: write strengths, positive. `log_decay`: log decays, negative.
All inputs are finite; a program needn't handle non-finite values.
Results may differ from a plain program's by a relative error of at most 0.022.
Values may be sent and summed in bfloat16 or wider, within the bound.
No kernel may reach another device: no remote copies, remote signals or barrier semaphores. Data moves between devices by JAX's collectives and lax.ppermute only.
A program may use at most 128 MiB of HBM per device.

v0:
```python
import jax
import jax.numpy as jnp
from jax import lax
from jax.sharding import PartitionSpec as P

DH = 128
WINDOW = 1024


highest = lax.Precision.HIGHEST


def carried_in(shard, axis, join, neutral):
    place = lax.axis_index(axis)
    gathered = jax.tree.map(
        lambda a, kind: lax.all_gather(a.astype(kind), axis),
        shard,
        jax.tree.map(lambda a: jnp.bfloat16 if a.dtype == jnp.float32 else a.dtype, shard),
    )
    state = jax.tree.map(lambda a, e: jnp.zeros_like(a) + jnp.asarray(e, a.dtype), shard, neutral)

    def one(turn, state):
        return join(
            state,
            jax.tree.map(
                lambda a, own: lax.dynamic_index_in_dim(a, turn, 0, False).astype(own.dtype),
                gathered,
                shard,
            ),
        )

    return lax.fori_loop(0, place, one, state)


def passed_along(block, axis, distance):
    devices = range(lax.axis_size(axis))
    route = [(i - distance, i) for i in devices if i - distance in devices]
    return lax.ppermute(block, axis, route)


def unit_rows(array):
    return array / jnp.sqrt(jnp.sum(array * array, axis=-1, keepdims=True) + 1e-06)


def unit_inverse(lower_part):
    order_len = lower_part.shape[-1]
    identity = jnp.eye(order_len, dtype=jnp.float32)
    powered = -lower_part
    result = identity + powered
    for counter in range(1, max(1, (order_len - 1).bit_length())):
        powered = jnp.matmul(powered, powered, precision=highest)
        result = jnp.matmul(result, identity + powered, precision=highest)
    return result


def block_terms(queries, keys_in, values_in, betas, log_rates):
    cumulative = jnp.cumsum(log_rates, axis=-1)
    length = queries.shape[-2]
    positions = jnp.arange(length)
    strict = positions[:, None] > positions[None, :]
    inclusive = positions[:, None] >= positions[None, :]
    spread = cumulative[..., :, None] - cumulative[..., None, :]
    ratio_strict = jnp.where(strict, jnp.exp(jnp.where(strict, spread, 0.0)), 0.0)
    ratio_incl = jnp.where(inclusive, jnp.exp(jnp.where(inclusive, spread, 0.0)), 0.0)
    key_gram = jnp.einsum("...td,...sd->...ts", keys_in, keys_in, precision=highest)
    inverse = unit_inverse(betas[..., :, None] * ratio_strict * key_gram)
    decayed = jnp.exp(cumulative)
    pseudo = jnp.matmul(inverse, betas[..., None] * values_in, precision=highest)
    writer = jnp.matmul(inverse, (betas * decayed)[..., None] * keys_in, precision=highest)
    to_end = jnp.exp(cumulative[..., -1:] - cumulative)
    keys_end = keys_in * to_end[..., None]
    identity = jnp.eye(queries.shape[-1], dtype=jnp.float32)
    transition = jnp.exp(cumulative[..., -1])[..., None, None] * identity - jnp.einsum(
        "...td,...te->...de", keys_end, writer, precision=highest
    )
    contrib = jnp.einsum("...td,...te->...de", keys_end, pseudo, precision=highest)
    mixing = ratio_incl * jnp.einsum("...td,...sd->...ts", queries, keys_in, precision=highest)
    local_out = jnp.matmul(mixing, pseudo, precision=highest)
    carry_out = decayed[..., None] * queries - jnp.matmul(mixing, writer, precision=highest)
    return (transition, contrib, local_out, carry_out)


def window_block(queries, keys_in, values_in, query_pos, key_pos):
    scores = jnp.einsum(
        "thd,shd->hts", queries, keys_in, preferred_element_type=jnp.float32
    ) * DH ** (-0.5)
    offsets = query_pos[:, None] - key_pos[None, :]
    inside = (offsets >= 0) & (offsets < WINDOW) & (key_pos[None, :] >= 0)
    masked = jnp.where(inside[None], scores, -1e30)
    block_max = jnp.max(masked, axis=-1)
    weights = jnp.where(inside[None], jnp.exp(masked - block_max[..., None]), 0.0)
    probs = weights.astype(jnp.bfloat16)
    block_num = jnp.einsum("hts,shd->htd", probs, values_in, preferred_element_type=jnp.float32)
    block_den = jnp.sum(weights, axis=-1)
    return (block_max, block_num, block_den)


def chain_pairs(earlier, later):
    matrix = jnp.einsum("hij,hjk->hik", later[0], earlier[0], precision=highest)
    vector = jnp.einsum("hij,hjk->hik", later[0], earlier[1], precision=highest) + later[1]
    return (matrix, vector)


def shards(
    delta_q,
    delta_k,
    delta_v,
    beta,
    log_decay,
    out_gate,
    norm_gain,
    attn_q,
    attn_k,
    attn_v,
    w_delta_out,
    w_attn_out,
):
    rows_here = delta_q.shape[0]
    local_heads = delta_q.shape[1] // DH
    block_len = min(64, rows_here)
    blocks = rows_here // block_len

    def heads_blocks(array):
        return (
            array.astype(jnp.float32)
            .reshape(blocks, block_len, local_heads, DH)
            .transpose(2, 0, 1, 3)
        )

    queries = unit_rows(heads_blocks(delta_q)) * DH ** (-0.5)
    keys_in = unit_rows(heads_blocks(delta_k))
    values_in = heads_blocks(delta_v)
    betas = beta.reshape(blocks, block_len, local_heads).transpose(2, 0, 1)
    log_rates = log_decay.reshape(blocks, block_len, local_heads).transpose(2, 0, 1)
    transition, contrib, local_out, carry_out = block_terms(
        queries, keys_in, values_in, betas, log_rates
    )
    identity = jnp.broadcast_to(jnp.eye(DH, dtype=jnp.float32), (local_heads, DH, DH))
    zero_state = jnp.zeros((local_heads, DH, DH), jnp.float32)

    def compose(carried, inputs):
        after_pair = chain_pairs(carried, inputs)
        return (after_pair, carried)

    shard_pair, starts = lax.scan(
        compose,
        (identity, zero_state),
        (transition.transpose(1, 0, 2, 3), contrib.transpose(1, 0, 2, 3)),
    )
    start_mats = starts[0].transpose(1, 0, 2, 3)
    start_vecs = starts[1].transpose(1, 0, 2, 3)
    own_out = local_out + jnp.einsum("hntd,hnde->hnte", carry_out, start_vecs, precision=highest)
    reach = jnp.einsum("hntd,hnde->hnte", carry_out, start_mats, precision=highest)
    prefix_pair = carried_in(shard_pair, "ctx", chain_pairs, (identity, zero_state))
    incoming_state = prefix_pair[1]
    delta_raw = own_out + jnp.einsum("hntd,hde->hnte", reach, incoming_state, precision=highest)
    delta_raw = delta_raw.transpose(1, 2, 0, 3).reshape(rows_here, local_heads, DH)
    gate_act = jax.nn.silu(out_gate.astype(jnp.float32).reshape(rows_here, local_heads, DH))
    normed = (
        delta_raw
        / jnp.sqrt(jnp.mean(delta_raw * delta_raw, axis=-1, keepdims=True) + 1e-06)
        * norm_gain
        * gate_act
    )
    delta_heads = normed.reshape(rows_here, local_heads * DH).astype(jnp.bfloat16)
    position = lax.axis_index("ctx")
    query_rows = attn_q.reshape(rows_here, local_heads, DH)
    query_pos = position * rows_here + jnp.arange(rows_here, dtype=jnp.int32)
    maxima, numers, denoms = ([], [], [])
    own_max, own_num, own_den = window_block(
        query_rows,
        attn_k.reshape(rows_here, local_heads, DH),
        attn_v.reshape(rows_here, local_heads, DH),
        query_pos,
        query_pos,
    )
    maxima.append(own_max)
    numers.append(own_num)
    denoms.append(own_den)
    for back in range(1, WINDOW // rows_here + 1):
        keys_far, values_far = passed_along((attn_k, attn_v), "ctx", back)
        key_pos = (position - back) * rows_here + jnp.arange(rows_here, dtype=jnp.int32)
        remote_maximum, far_num, far_den = window_block(
            query_rows,
            keys_far.reshape(rows_here, local_heads, DH),
            values_far.reshape(rows_here, local_heads, DH),
            query_pos,
            key_pos,
        )
        maxima.append(remote_maximum)
        numers.append(far_num)
        denoms.append(far_den)
    top = maxima[0]
    for block_max in maxima[1:]:
        top = jnp.maximum(top, block_max)
    numer = jnp.zeros_like(numers[0])
    denom = jnp.zeros_like(denoms[0])
    for block_max, block_num, block_den in zip(maxima, numers, denoms):
        factor = jnp.exp(block_max - top)
        numer = numer + factor[..., None] * block_num
        denom = denom + factor * block_den
    attn_heads = (
        (numer / denom[..., None])
        .transpose(1, 0, 2)
        .reshape(rows_here, local_heads * DH)
        .astype(jnp.bfloat16)
    )
    running_partial_sum = jnp.dot(delta_heads, w_delta_out, preferred_element_type=jnp.float32)
    running_partial_sum = running_partial_sum + jnp.dot(
        attn_heads, w_attn_out, preferred_element_type=jnp.float32
    )
    total = lax.psum_scatter(
        running_partial_sum.astype(jnp.bfloat16), "head", scatter_dimension=0, tiled=True
    )
    return total


def solution(mesh):
    return jax.shard_map(
        shards,
        mesh=mesh,
        in_specs=(
            P("ctx", "head"),
            P("ctx", "head"),
            P("ctx", "head"),
            P("ctx", "head"),
            P("ctx", "head"),
            P("ctx", "head"),
            P(),
            P("ctx", "head"),
            P("ctx", "head"),
            P("ctx", "head"),
            P("head", None),
            P("head", None),
        ),
        out_specs=P(("ctx", "head"), None),
        check_vma=False,
    )
```

profile of v0, /device:TPU:160, one launch (start us, length us, event | category | flops | bytes accessed | tf_op | source)
XLA Modules:
  0.0 349.2 jit_solution(1024189018502557563)
XLA Ops:
  8.6 1.3 reshape.511
  20.6 1.9 reshape.512
  23.2 2.0 fusion.77
  26.7 3.1 convolution_bitcast_fusion
  29.8 3.3 fusion.15
  33.2 14.9 %while.30 = (s32[]{:T(128)}, f32[4,128,128]{2,1,0:T(8,128)S(1)}, f32[4,128,128]{2,1,0:T(8,128)S(1)}, f32[4,4,128,128]{3,2,1,0:T(8,128)}, f32[4,4,128,128]{3,2,1,...) while((s32[]{:T(128)}, f32[4,128,128]{2,1,0:T(8,128)S(1)}, ...), condition=%wide.region_4.5_spmd.clone, body=%wide.region_3.4_spmd.clone.sunk | while | flops 201523200 | bytes 3933815 | solution.py:145
  34.1 1.3 fusion.229
  35.4 1.4 convolution_add_fusion.8
  37.8 1.3 fusion.229
  39.2 1.4 convolution_add_fusion.8
  41.6 1.3 fusion.229
  42.9 1.4 convolution_add_fusion.8
  45.3 1.3 fusion.229
  46.6 1.4 convolution_add_fusion.8
  49.6 1.8 copy.76
  51.5 5.1 %collective-permute-start.3 = (bf16[256,512]{0,1:T(8,128)(2,1)}, bf16[256,512]{0,1:T(8,128)(2,1)}, u32[]{:S(2)}, u32[]{:S(2)}) collective-permute-start(bf16[256,512]{0,1:T(8,128)(2,1)} %copy.76), channel_id=1, source_target_pairs={{0,16},{4,20},{8,24},{12,28},{16,32},{20,36},{24,40},{28,44},{32,4... | collective-permute-start | bytes 786440 | tf_op jit(solution)/shard_map/ppermute | solution.py:38
  56.6 2.6 collective-permute-start.1
  59.2 1.9 collective-permute-start.2
  61.1 4.3 %collective-permute-start = (bf16[256,512]{0,1:T(8,128)(2,1)}, bf16[256,512]{0,1:T(8,128)(2,1)}, u32[]{:S(2)}, u32[]{:S(2)}) collective-permute-start(bf16[256,512]{0,1:T(8,128)(2,1)} %copy.76), channel_id=1, source_target_pairs={{0,4},{4,8},{8,12},{12,16},{16,20},{20,24},{24,28},{28,32},{32,36}... | collective-permute-start | bytes 786440 | tf_op jit(solution)/shard_map/ppermute | solution.py:38
  65.4 3.6 %collective-permute-start.7 = (bf16[256,512]{1,0:T(8,128)(2,1)}, bf16[256,512]{1,0:T(8,128)(2,1)}, u32[]{:S(2)}, u32[]{:S(2)}) collective-permute-start(bf16[256,512]{1,0:T(8,128)(2,1)} %param.25), channel_id=1, source_target_pairs={{0,16},{4,20},{8,24},{12,28},{16,32},{20,36},{24,40},{28,44},{32,4... | collective-permute-start | bytes 786440 | tf_op jit(solution)/shard_map/ppermute | solution.py:38
  69.0 1.8 copy.109
  73.3 2.3 fusion.161
  75.6 1.9 convolution_multiply_fusion.6
  78.8 1.9 fusion.35
  80.6 1.4 fusion.167
  82.1 1.9 collective-permute-start.6
  84.0 1.3 fusion.157
  85.4 3.5 %collective-permute-start.5 = (bf16[256,512]{1,0:T(8,128)(2,1)}, bf16[256,512]{1,0:T(8,128)(2,1)}, u32[]{:S(2)}, u32[]{:S(2)}) collective-permute-start(bf16[256,512]{1,0:T(8,128)(2,1)} %param.25), channel_id=1, source_target_pairs={{0,8},{4,12},{8,16},{12,20},{16,24},{20,28},{24,32},{28,36},{32,40... | collective-permute-start | bytes 786440 | tf_op jit(solution)/shard_map/ppermute | solution.py:38
  88.9 1.3 fusion.159
  90.2 4.2 %collective-permute-start.4 = (bf16[256,512]{1,0:T(8,128)(2,1)}, bf16[256,512]{1,0:T(8,128)(2,1)}, u32[]{:S(2)}, u32[]{:S(2)}) collective-permute-start(bf16[256,512]{1,0:T(8,128)(2,1)} %param.25), channel_id=1, source_target_pairs={{0,4},{4,8},{8,12},{12,16},{16,20},{20,24},{24,28},{28,32},{32,36}... | collective-permute-start | bytes 786440 | tf_op jit(solution)/shard_map/ppermute | solution.py:38
  94.5 2.3 fusion.158
  97.6 1.8 copy.96
  99.4 1.8 copy.94
  101.2 1.9 collective-permute-done.5
  103.1 1.8 copy.92
  104.9 1.5 collective-permute-done.4
  106.4 1.8 copy.90
  108.2 1.7 fusion.42
  110.0 1.4 fusion.160
  115.1 30.2 %all-gather.5.cloned.1.call-done = bf16[256,128,128]{2,1,0:T(8,128)(2,1)} async-done(((bf16[4,128,128]{2,1,0:T(8,128)(2,1)}), bf16[256,128,128]{2,1,0:T(8,128)(2,1)}) %all-gather.5.cloned.1.call-update) | async-done | bytes 8388624 | tf_op jit(solution)/shard_map/all_gather | solution.py:16
  145.2 82.6 %all-gather.7.cloned.1.call-done = bf16[256,128,128]{2,1,0:T(8,128)(2,1)} async-done(((bf16[4,128,128]{2,1,0:T(8,128)(2,1)}), bf16[256,128,128]{2,1,0:T(8,128)(2,1)}) %all-gather.7.cloned.1.call-update) | async-done | bytes 8388624 | tf_op jit(solution)/shard_map/all_gather | solution.py:16
  227.9 52.5 %while.29 = (s32[]{:T(128)}, f32[4,128,128]{2,1,0:T(8,128)S(1)}, s32[]{:T(128)}, bf16[64,4,128,128]{3,2,1,0:T(8,128)(2,1)}, bf16[64,4,128,128]{3,2,1,0:T(8,128)(2,1)}, /*index=5*/s32[]{:T(128)}, s32[]{:T(128)}, s32[]{:T(128)}) while((s32[]{:T(128)}, f32[4,128,128]{2,1,0:T(8,128)S(1)}, s32[]{:T(128)}, bf16[64,4,128,128]{3,2,1,0:T(8,128)(2,1)}, ...), condition=%wide.region_6.7_spmd, body=%wide.region_5.6_spmd.sunk | while | flops 100794368 | bytes 1311871 | solution.py:32
  227.9 1.3 convolution_add_fusion.7
  272.6 1.3 convolution_add_fusion.7
  280.4 1.6 fusion.106
  282.1 2.6 multiply_reduce_fusion
  287.1 1.7 fusion.14
  288.9 53.8 %reduce-scatter.2.cloned.1.call-done = bf16[64,2048]{1,0:T(8,128)(2,1)} async-done(((bf16[256,2048]{1,0:T(8,128)(2,1)}), bf16[64,2048]{1,0:T(8,128)(2,1)}) %reduce-scatter.2.cloned.1.call-update) | async-done | bytes 262160 | tf_op jit(solution)/shard_map/reduce_scatter | solution.py:212
  (245 shorter events, 78.7 us)
Async XLA Ops:
  6.5 278.9 %copy-start = (bf16[512,2048]{1,0:T(8,128)(2,1)S(1)}, bf16[512,2048]{1,0:T(8,128)(2,1)}, u32[]{:S(2)}) copy-start(bf16[512,2048]{1,0:T(8,128)(2,1)} %param.26) | copy-start | bytes 6291460
  6.5 3.9 %copy-start.35 = (f32[256,4]{0,1:T(4,128)S(1)}, f32[256,4]{0,1:T(4,128)}, u32[]{:S(2)}) copy-start(f32[256,4]{0,1:T(4,128)} %param.19) | copy-start | bytes 12292
  6.5 138.7 %all-gather.5.cloned.1.call-start = ((), (), s32[]{:S(2)}) async-start(), calls=%async_computation.2 | async-start | bytes 8519680 | tf_op jit(solution)/shard_map/all_gather | solution.py:16
  8.6 6.0 %copy-start.10 = (f32[4,64,4,128]{3,2,1,0:T(4,128)}, f32[4,64,4,128]{3,2,1,0:T(4,128)S(1)}, u32[]{:S(2)}) copy-start(f32[4,64,4,128]{3,2,1,0:T(4,128)S(1)} %reshape.510) | copy-start | bytes 1572868
  10.0 8.7 %copy-start.12 = (f32[4,64,4,128]{3,2,1,0:T(4,128)}, f32[4,64,4,128]{3,2,1,0:T(4,128)S(1)}, u32[]{:S(2)}) copy-start(f32[4,64,4,128]{3,2,1,0:T(4,128)S(1)} %reshape.511) | copy-start | bytes 1572868
  13.5 16.3 %copy-start.32 = (f32[4,4,64]{2,1,0:T(4,128)}, f32[4,4,64]{2,1,0:T(4,128)S(1)}, u32[]{:S(2)}) copy-start(f32[4,4,64]{2,1,0:T(4,128)S(1)} %get-tuple-element.191) | copy-start | bytes 12292
  19.9 3.3 copy-start.34
  22.5 2.7 copy-start.8
  23.2 3.5 %copy-start.13 = (f32[4,64,4,128]{3,2,1,0:T(4,128)S(1)}, f32[4,64,4,128]{3,2,1,0:T(4,128)}, u32[]{:S(2)}) copy-start(f32[4,64,4,128]{3,2,1,0:T(4,128)} %copy-done.12) | copy-start | bytes 1572868
  23.2 3.5 %copy-start.33 = (f32[4,4,64]{2,1,0:T(4,128)S(1)}, f32[4,4,64]{2,1,0:T(4,128)}, u32[]{:S(2)}) copy-start(f32[4,4,64]{2,1,0:T(4,128)} %get-tuple-element.171) | copy-start | bytes 12292
  25.2 4.6 %copy-start.40 = (f32[4,4,64,128]{3,2,1,0:T(8,128)}, f32[4,4,64,128]{3,2,1,0:T(8,128)S(1)}, u32[]{:S(2)}) copy-start(f32[4,4,64,128]{3,2,1,0:T(8,128)S(1)} %fusion.77) | copy-start | bytes 1572868
  25.2 4.6 %copy-start.37 = (f32[4,4]{0,1:T(4,128)S(1)}, f32[4,4]{0,1:T(4,128)}, u32[]{:S(2)}) copy-start(f32[4,4]{0,1:T(4,128)} %exponential_bitcast_fusion) | copy-start | bytes 196
  48.1 22.9 %copy-start.38 = (f32[128]{0:T(128)S(1)}, f32[128]{0:T(128)}, u32[]{:S(2)}) copy-start(f32[128]{0:T(128)} %param.22) | copy-start | bytes 1540
  48.1 25.2 %copy-start.4 = (bf16[256,512]{1,0:T(8,128)(2,1)S(1)}, bf16[256,512]{1,0:T(8,128)(2,1)}, u32[]{:S(2)}) copy-start(bf16[256,512]{1,0:T(8,128)(2,1)} %param.23) | copy-start | bytes 786436
  48.1 27.5 %copy-start.11 = (f32[4,64,4,128]{3,2,1,0:T(4,128)S(1)}, f32[4,64,4,128]{3,2,1,0:T(4,128)}, u32[]{:S(2)}) copy-start(f32[4,64,4,128]{3,2,1,0:T(4,128)} %copy-done.10) | copy-start | bytes 1572868
  48.8 179.0 %all-gather.7.cloned.1.call-start = ((), (), s32[]{:S(2)}) async-start(), calls=%async_computation.3 | async-start | bytes 8519680 | tf_op jit(solution)/shard_map/all_gather | solution.py:16
  49.5 26.0 %copy-start.14 = (f32[4,64,4,128]{3,2,1,0:T(4,128)S(1)}, f32[4,64,4,128]{3,2,1,0:T(4,128)}, u32[]{:S(2)}) copy-start(f32[4,64,4,128]{3,2,1,0:T(4,128)} %copy-done.12) | copy-start | bytes 1572868
  49.6 293.1 %reduce-scatter.2.cloned.1.call-start = ((), (), s32[]{:S(2)}) async-start(), calls=%async_computation.1 | async-start | bytes 1310720 | tf_op jit(solution)/shard_map/reduce_scatter | solution.py:212
  51.5 30.6 %collective-permute-start.3 = (bf16[256,512]{0,1:T(8,128)(2,1)}, bf16[256,512]{0,1:T(8,128)(2,1)}, u32[]{:S(2)}, u32[]{:S(2)}) collective-permute-start(bf16[256,512]{0,1:T(8,128)(2,1)} %copy.76), channel_id=1, source_target_pairs={{0,16},{4,20},{8,24},{12,28},{16,32},{20,36},{24,40},{28,44},{32,4... | collective-permute-start | bytes 786440 | tf_op jit(solution)/shard_map/ppermute | solution.py:38
  56.6 28.8 %collective-permute-start.1 = (bf16[256,512]{0,1:T(8,128)(2,1)}, bf16[256,512]{0,1:T(8,128)(2,1)}, u32[]{:S(2)}, u32[]{:S(2)}) collective-permute-start(bf16[256,512]{0,1:T(8,128)(2,1)} %copy.76), channel_id=1, source_target_pairs={{0,8},{4,12},{8,16},{12,20},{16,24},{20,28},{24,32},{28,36},{32,40... | collective-permute-start | bytes 786440 | tf_op jit(solution)/shard_map/ppermute | solution.py:38
  59.2 31.1 %collective-permute-start.2 = (bf16[256,512]{0,1:T(8,128)(2,1)}, bf16[256,512]{0,1:T(8,128)(2,1)}, u32[]{:S(2)}, u32[]{:S(2)}) collective-permute-start(bf16[256,512]{0,1:T(8,128)(2,1)} %copy.76), channel_id=1, source_target_pairs={{0,12},{4,16},{8,20},{12,24},{16,28},{20,32},{24,36},{28,40},{32,4... | collective-permute-start | bytes 786440 | tf_op jit(solution)/shard_map/ppermute | solution.py:38
  61.1 48.9 %collective-permute-start = (bf16[256,512]{0,1:T(8,128)(2,1)}, bf16[256,512]{0,1:T(8,128)(2,1)}, u32[]{:S(2)}, u32[]{:S(2)}) collective-permute-start(bf16[256,512]{0,1:T(8,128)(2,1)} %copy.76), channel_id=1, source_target_pairs={{0,4},{4,8},{8,12},{12,16},{16,20},{20,24},{24,28},{28,32},{32,36}... | collective-permute-start | bytes 786440 | tf_op jit(solution)/shard_map/ppermute | solution.py:38
  65.4 32.2 %collective-permute-start.7 = (bf16[256,512]{1,0:T(8,128)(2,1)}, bf16[256,512]{1,0:T(8,128)(2,1)}, u32[]{:S(2)}, u32[]{:S(2)}) collective-permute-start(bf16[256,512]{1,0:T(8,128)(2,1)} %param.25), channel_id=1, source_target_pairs={{0,16},{4,20},{8,24},{12,28},{16,32},{20,36},{24,40},{28,44},{32,4... | collective-permute-start | bytes 786440 | tf_op jit(solution)/shard_map/ppermute | solution.py:38
  72.7 24.1 %copy-start.22 = (pred[256,256]{0,1:T(8,128)(4,1)}, pred[256,256]{0,1:T(8,128)(4,1)S(1)}, u32[]{:S(2)}) copy-start(pred[256,256]{0,1:T(8,128)(4,1)S(1)} %get-tuple-element.176) | copy-start | bytes 196612
  75.6 2.0 copy-start.30
  75.6 2.0 copy-start.31
  75.6 2.0 copy-start.41
  77.5 1.2 copy-start.17
  77.6 3.1 copy-start.7
  78.3 5.7 %copy-start.16 = (f32[4,4,64,128]{3,2,1,0:T(8,128)}, f32[4,4,64,128]{3,2,1,0:T(8,128)S(1)}, u32[]{:S(2)}) copy-start(f32[4,4,64,128]{3,2,1,0:T(8,128)S(1)} %convolution_subtract_fusion) | copy-start | bytes 1572868
  82.1 17.3 %collective-permute-start.6 = (bf16[256,512]{1,0:T(8,128)(2,1)}, bf16[256,512]{1,0:T(8,128)(2,1)}, u32[]{:S(2)}, u32[]{:S(2)}) collective-permute-start(bf16[256,512]{1,0:T(8,128)(2,1)} %param.25), channel_id=1, source_target_pairs={{0,12},{4,16},{8,20},{12,24},{16,28},{20,32},{24,36},{28,40},{32,4... | collective-permute-start | bytes 786440 | tf_op jit(solution)/shard_map/ppermute | solution.py:38
  85.3 12.3 %copy-start.1 = (f32[4,256,256]{1,2,0:T(8,128)}, f32[4,256,256]{1,2,0:T(8,128)S(1)}, u32[]{:S(2)}) copy-start(f32[4,256,256]{1,2,0:T(8,128)S(1)} %get-tuple-element.182) | copy-start | bytes 3145732
  85.4 17.8 %collective-permute-start.5 = (bf16[256,512]{1,0:T(8,128)(2,1)}, bf16[256,512]{1,0:T(8,128)(2,1)}, u32[]{:S(2)}, u32[]{:S(2)}) collective-permute-start(bf16[256,512]{1,0:T(8,128)(2,1)} %param.25), channel_id=1, source_target_pairs={{0,8},{4,12},{8,16},{12,20},{16,24},{20,28},{24,32},{28,36},{32,40... | collective-permute-start | bytes 786440 | tf_op jit(solution)/shard_map/ppermute | solution.py:38
  90.2 16.2 %collective-permute-start.4 = (bf16[256,512]{1,0:T(8,128)(2,1)}, bf16[256,512]{1,0:T(8,128)(2,1)}, u32[]{:S(2)}, u32[]{:S(2)}) collective-permute-start(bf16[256,512]{1,0:T(8,128)(2,1)} %param.25), channel_id=1, source_target_pairs={{0,4},{4,8},{8,12},{12,16},{16,20},{20,24},{24,28},{28,32},{32,36}... | collective-permute-start | bytes 786440 | tf_op jit(solution)/shard_map/ppermute | solution.py:38
  108.2 1.8 copy-start.24
  108.2 3.2 copy-start.5
  108.2 3.2 copy-start.26
  109.9 1.9 copy-start.29
  109.9 2.0 copy-start.2
  109.9 2.0 copy-start.21
  109.9 2.0 copy-start.23
  111.4 1.2 copy-start.3
  111.4 1.3 copy-start.20
  227.9 54.2 %copy-start.15 = (f32[4,4,64,128]{3,2,1,0:T(8,128)S(1)}, f32[4,4,64,128]{3,2,1,0:T(8,128)}, u32[]{:S(2)}) copy-start(f32[4,4,64,128]{3,2,1,0:T(8,128)} %fusion.167) | copy-start | bytes 1572868
  282.1 3.4 copy-start.36
  282.1 3.4 copy-start.39
  285.5 1.6 copy-start.9
  285.5 1.6 copy-start.28
  (5 other events, 4.7 us)
Sparse Core Ops, SparseCore 0:
  48.9 96.2 all-gather.4
  148.0 79.7 all-gather.6
  289.0 53.6 reduce-scatter.1
where the time goes:
time: 353 us; the launch traced here: 349 us
  waiting for transfers between devices  170 us (48%)
  matrix products  102 us (29%)
  starting transfers between devices  27.2 us (8%)
  local copies, waits for them, and re-layouts  22.7 us (6%)
  between operations  14 us (4%)
  other arithmetic  11.7 us (3%)
    all_gather x2, waiting for transfers between devices, carried_in(): lax.all_gather(a.astype(kind), axis)  113 us
    dot_general x44, matrix products, chain_pairs(): jnp.einsum('hij,hjk->hik', later[0], earlier[1], precision=highest)  56 us
    reduce_scatter x1, waiting for transfers between devices, shards(): lax.psum_scatter(running_partial_sum.astype(jnp.bfloat16), 'head', scatte...  53.8 us
    ppermute x8, starting transfers between devices, passed_along(): return lax.ppermute(block, axis, route)  27.2 us
    dot_general x5, matrix products, window_block(): jnp.einsum('thd,shd->hts', queries, keys_in, preferred_element_type=jnp.f...  8.65 us
    ppermute x4, local copies, waits for them, and re-layouts, passed_along(): return lax.ppermute(block, axis, route)  7.19 us
  transfers between devices with their start and end apart: 11, of which 5 were waited for; matrix products, arithmetic and copies ran while one was open for 10% of the time, Pallas kernels for 0%

commit v1 on v0

--- a/solution.py
+++ b/solution.py
@@ -10,26 +10,24 @@
 highest = lax.Precision.HIGHEST
 
 
-def carried_in(shard, axis, join, neutral):
+def prefix_state(pair, axis):
     place = lax.axis_index(axis)
-    gathered = jax.tree.map(
-        lambda a, kind: lax.all_gather(a.astype(kind), axis),
-        shard,
-        jax.tree.map(lambda a: jnp.bfloat16 if a.dtype == jnp.float32 else a.dtype, shard),
-    )
-    state = jax.tree.map(lambda a, e: jnp.zeros_like(a) + jnp.asarray(e, a.dtype), shard, neutral)
-
-    def one(turn, state):
-        return join(
-            state,
-            jax.tree.map(
-                lambda a, own: lax.dynamic_index_in_dim(a, turn, 0, False).astype(own.dtype),
-                gathered,
-                shard,
-            ),
-        )
-
-    return lax.fori_loop(0, place, one, state)
+    size = lax.axis_size(axis)
+    mat, vec = pair
+    distance = 1
+    while distance < size:
+        if 2 * distance >= size:
+            far_vec = passed_along(vec.astype(jnp.bfloat16), axis, distance).astype(jnp.float32)
+            vec = jnp.einsum("hij,hjk->hik", mat, far_vec, precision=highest) + vec
+        else:
+            far_mat, far_vec = passed_along(
+                (mat.astype(jnp.bfloat16), vec.astype(jnp.bfloat16)), axis, distance
+            )
+            joined = chain_pairs((far_mat.astype(jnp.float32), far_vec.astype(jnp.float32)), (mat, vec))
+            mat = jnp.where(place >= distance, joined[0], mat)
+            vec = jnp.where(place >= distance, joined[1], vec)
+        distance *= 2
+    return passed_along(vec.astype(jnp.bfloat16), axis, 1).astype(jnp.float32)
 
 
 def passed_along(block, axis, distance):
@@ -151,8 +149,7 @@
     start_vecs = starts[1].transpose(1, 0, 2, 3)
     own_out = local_out + jnp.einsum("hntd,hnde->hnte", carry_out, start_vecs, precision=highest)
     reach = jnp.einsum("hntd,hnde->hnte", carry_out, start_mats, precision=highest)
-    prefix_pair = carried_in(shard_pair, "ctx", chain_pairs, (identity, zero_state))
-    incoming_state = prefix_pair[1]
+    incoming_state = prefix_state(shard_pair, "ctx")
     delta_raw = own_out + jnp.einsum("hntd,hde->hnte", reach, incoming_state, precision=highest)
     delta_raw = delta_raw.transpose(1, 2, 0, 3).reshape(rows_here, local_heads, DH)
     gate_act = jax.nn.silu(out_gate.astype(jnp.float32).reshape(rows_here, local_heads, DH))
@@ -209,10 +206,12 @@
     running_partial_sum = running_partial_sum + jnp.dot(
         attn_heads, w_attn_out, preferred_element_type=jnp.float32
     )
-    total = lax.psum_scatter(
-        running_partial_sum.astype(jnp.bfloat16), "head", scatter_dimension=0, tiled=True
-    )
-    return total
+    n_head = lax.axis_size("head")
+    pieces = lax.all_to_all(
+        running_partial_sum.astype(jnp.bfloat16), "head", 0, 0, tiled=True
+    )
+    pieces = pieces.reshape(n_head, rows_here // n_head, pieces.shape[-1]).astype(jnp.float32)
+    return jnp.sum(pieces, axis=0).astype(jnp.bfloat16)
 
 
 def solution(mesh):

time: 353 us -> 212 us (0.60)
  waiting for transfers between devices: 170 us -> 46.8 us
  matrix products: 102 us -> 63.7 us
  starting transfers between devices: 27.2 us -> 54.1 us
  blocking collectives: 0 us -> 15 us
  between operations: 14 us -> 1.11 us
  local copies, waits for them, and re-layouts: 22.7 us -> 18.8 us
    all_gather x2 -> x0, waiting for transfers between devices: 113 us -> none  [carried_in(): lax.all_gather(a.astype(kind), axis)]
    reduce_scatter x1 -> x0, waiting for transfers between devices: 53.8 us -> none  [shards(): lax.psum_scatter(running_partial_sum.astype(jnp.bfloat16), 'head', scatte...]
    dot_general x44 -> x9, matrix products: 56 us -> 8.72 us  [chain_pairs(): jnp.einsum('hij,hjk->hik', later[0], earlier[1], precision=highest)]
    ppermute x8 -> x20, waiting for transfers between devices: 3.41 us -> 46.8 us  [passed_along(): return lax.ppermute(block, axis, route)]
    ppermute x8 -> x20, starting transfers between devices: 27.2 us -> 54.1 us  [passed_along(): return lax.ppermute(block, axis, route)]
    all_to_all x0 -> x1, blocking collectives: none -> 15 us  [shards(): lax.all_to_all(running_partial_sum.astype(jnp.bfloat16), 'head', 0, 0, ti...]
    dot_general x5, matrix products: 2.41 us -> 8.65 us  [window_block(): jnp.einsum('hts,shd->htd', probs, values_in, preferred_element_type=jnp.f...]
    dot_general x5, matrix products: 8.65 us -> 4.65 us  [window_block(): jnp.einsum('thd,shd->hts', queries, keys_in, preferred_element_type=jnp.f...]
  transfers between devices with their start and end apart: 11 -> 20, of which waited for: 5 -> 9; matrix products, arithmetic and copies ran while one was open for 10% -> 41% of each run, Pallas kernels for 0% -> 0%
where the time goes in v1:
time: 212 us; the launch traced here: 210 us
  matrix products  63.7 us (30%)
  starting transfers between devices  54.1 us (26%)
  waiting for transfers between devices  46.8 us (22%)
  local copies, waits for them, and re-layouts  18.8 us (9%)
  blocking collectives  15 us (7%)
  other arithmetic  10.6 us (5%)
    ppermute x20, starting transfers between devices, passed_along(): return lax.ppermute(block, axis, route)  54.1 us
    ppermute x20, waiting for transfers between devices, passed_along(): return lax.ppermute(block, axis, route)  46.8 us
    all_to_all x1, blocking collectives, shards(): lax.all_to_all(running_partial_sum.astype(jnp.bfloat16), 'head', 0, 0, ti...  15 us
    dot_general x9, matrix products, chain_pairs(): matrix = jnp.einsum('hij,hjk->hik', later[0], earlier[0], precision=highest)  9.12 us
    dot_general x9, matrix products, chain_pairs(): jnp.einsum('hij,hjk->hik', later[0], earlier[1], precision=highest)  8.72 us
    dot_general x5, matrix products, window_block(): jnp.einsum('hts,shd->htd', probs, values_in, preferred_element_type=jnp.f...  8.65 us
    ppermute x4, local copies, waits for them, and re-layouts, passed_along(): return lax.ppermute(block, axis, route)  6.47 us
    dot_general x5, matrix products, window_block(): jnp.einsum('thd,shd->hts', queries, keys_in, preferred_element_type=jnp.f...  4.65 us
  transfers between devices with their start and end apart: 20, of which 9 were waited for; matrix products, arithmetic and copies ran while one was open for 41% of the time, Pallas kernels for 0%

profile of v1, /device:TPU:160, one launch (start us, length us, event | category | flops | bytes accessed | tf_op | source)
XLA Modules:
  0.0 210.3 jit_solution(2765104313279946322)
XLA Ops:
  0.0 2.0 copy.76
  2.0 5.1 %collective-permute-start.15 = (bf16[256,512]{0,1:T(8,128)(2,1)}, bf16[256,512]{0,1:T(8,128)(2,1)}, u32[]{:S(2)}, u32[]{:S(2)}) collective-permute-start(bf16[256,512]{0,1:T(8,128)(2,1)} %copy.76), channel_id=1, source_target_pairs={{0,16},{4,20},{8,24},{12,28},{16,32},{20,36},{24,40},{28,44},{32,4... | collective-permute-start | bytes 786440 | tf_op jit(solution)/shard_map/ppermute | solution.py:36
  7.1 2.6 %collective-permute-start.13 = (bf16[256,512]{0,1:T(8,128)(2,1)}, bf16[256,512]{0,1:T(8,128)(2,1)}, u32[]{:S(2)}, u32[]{:S(2)}) collective-permute-start(bf16[256,512]{0,1:T(8,128)(2,1)} %copy.76), channel_id=1, source_target_pairs={{0,8},{4,12},{8,16},{12,20},{16,24},{20,28},{24,32},{28,36},{32,40... | collective-permute-start | bytes 786440 | tf_op jit(solution)/shard_map/ppermute | solution.py:36
  9.7 1.9 collective-permute-start.14
  25.5 1.9 reshape.513
  28.1 1.7 fusion.65
  29.9 1.6 fusion.79
  31.6 4.2 %convolution_bitcast_fusion = f32[4,4,128,128]{3,2,0,1:T(8,128)} fusion(f32[4,4,64,128]{3,2,1,0:T(8,128)S(1)} %fusion.65, f32[4,4,64]{2,1,0:T(4,128)S(1)} %copy-done.35, f32[4,64,4,128]{3,2,1,0:T(4,128)} %copy-done.13, f32[4,4,64]{2,1,0:T(4,128)S(1)} %copy-done.34), kind=kOutput, calls=%fused_computation.16 | convolution fusion | flops 201588736 | bytes 2105344 | tf_op jit(solution)/shard_map/...td,...te->...de/dot_general | solution.py:74
  35.8 4.3 %fusion.12 = f32[4,4,128,128]{3,2,0,1:T(8,128)} fusion(f32[4,4,64,128]{3,2,1,0:T(8,128)S(1)} %copy-done.44, f32[128,128]{1,0:T(8,128)S(1)} %fusion.135, f32[4,4]{0,1:T(4,128)S(1)} %copy-done.41, f32[4,4,64]{2,1,0:T(4,128)S(1)} %copy-done.35, f32[4,64,4,128]{3,2,1,0:T(4,128)} %copy-done.13, f32[4,4,64]{2,1,0:T(4,128)S(1)} %copy-done.34), kind=kOutput, calls=%fused_computation.18 | convolution fusion | flops 202113024 | bytes 2170944 | tf_op jit(solution)/shard_map/...td,...te->...de/dot_general | solution.py:71
  40.1 14.9 %while.17 = (s32[]{:T(128)}, f32[4,128,128]{2,1,0:T(8,128)S(1)}, f32[4,128,128]{2,1,0:T(8,128)S(1)}, f32[4,4,128,128]{3,2,1,0:T(8,128)}, f32[4,4,128,128]{3,2,1,...) while((s32[]{:T(128)}, f32[4,128,128]{2,1,0:T(8,128)S(1)}, ...), condition=%wide.region_4.5_spmd.clone, body=%wide.region_3.4_spmd.clone.sunk | while | flops 201523200 | bytes 3933815 | solution.py:143
  46.1 1.4 convolution_add_fusion.12
  49.9 1.4 convolution_add_fusion.12
  55.7 4.3 %collective-permute-start = (bf16[4,128,128]{2,1,0:T(8,128)(2,1)}, bf16[4,128,128]{2,1,0:T(8,128)(2,1)}, u32[]{:S(2)}, u32[]{:S(2)}) collective-permute-start(bf16[4,128,128]{2,1,0:T(8,128)(2,1)} %convert_element_type.112), channel_id=1, source_target_pairs={{0,4},{4,8},{8,12},{12,16},{16,20},{20,24},{24,28},{28,32},{32,36}... | collective-permute-start | bytes 393224 | tf_op jit(solution)/shard_map/ppermute | solution.py:36
  60.0 3.6 %collective-permute-start.19 = (bf16[256,512]{1,0:T(8,128)(2,1)}, bf16[256,512]{1,0:T(8,128)(2,1)}, u32[]{:S(2)}, u32[]{:S(2)}) collective-permute-start(bf16[256,512]{1,0:T(8,128)(2,1)} %param.23), channel_id=1, source_target_pairs={{0,16},{4,20},{8,24},{12,28},{16,32},{20,36},{24,40},{28,44},{32,4... | collective-permute-start | bytes 786440 | tf_op jit(solution)/shard_map/ppermute | solution.py:36
  63.8 1.8 copy.109
  65.6 2.4 %convolution_multiply_fusion.6 = f32[4,4,64,64]{3,2,1,0:T(8,128)S(1)} fusion(f32[4,4,64]{2,1,0:T(4,128)S(1)} %reduce_window_sum.11, pred[64,64]{1,0:T(8,128)(4,1)S(1)} %iota_compare_fusion.3, f32[4,64,4,128]{3,2,1,0:T(4,128)} %copy-done.11, f32[4,4,64]{2,1,0:T(4,128)S(1)} %copy-done.32, f32[4,64,4,128]{3,2,1,0:T(4,128)} %copy-done.13, ...), kind=kOutput, calls=%fused_computation.39 | convolution fusion | flops 101318656 | bytes 1327104 | tf_op jit(solution)/shard_map/...td,...sd->...ts/dot_general | solution.py:75
  68.0 1.5 fusion.177
  69.5 1.5 convolution_subtract_fusion
  71.7 3.4 %fusion.37 = f32[4,4,64,128]{3,2,1,0:T(8,128)} fusion(f32[4,4,64,128]{3,2,1,0:T(8,128)} %convolution_subtract_fusion, f32[4,4,128,128]{3,2,1,0:T(8,128)} %get-tuple-element.46), kind=kOutput, calls=%fused_computation.70 | convolution fusion | flops 201326592 | bytes 2097152 | tf_op jit(solution)/shard_map/hntd,hnde->hnte/dot_general | solution.py:151
  75.1 1.9 convolution_add_fusion.2
  78.6 2.1 %collective-permute-start.5 = (bf16[4,128,128]{2,1,0:T(8,128)(2,1)S(1)}, bf16[4,128,128]{2,1,0:T(8,128)(2,1)S(1)}, u32[]{:S(2)}, u32[]{:S(2)}) collective-permute-start(bf16[4,128,128]{2,1,0:T(8,128)(2,1)S(1)} %copy-done.28), channel_id=1, source_target_pairs={{0,4},{4,8},{8,12},{12,16},{16,20},{20,24},{24,28},{28,32},{32,36}... | collective-permute-start | bytes 393224 | tf_op jit(solution)/shard_map/ppermute | solution.py:36
  81.9 5.1 %collective-permute-done.5 = bf16[4,128,128]{2,1,0:T(8,128)(2,1)S(1)} collective-permute-done((bf16[4,128,128]{2,1,0:T(8,128)(2,1)S(1)}, bf16[4,128,128]{2,1,0:T(8,128)(2,1)S(1)}, u32[]{:S(2)}, u32[]{:S(2)}) %collective-permute-start.5) | collective-permute-done | bytes 131104 | tf_op jit(solution)/shard_map/ppermute | solution.py:36
  87.0 1.9 collective-permute-start.12
  89.2 1.9 collective-permute-start.18
  92.4 3.9 %collective-permute-start.17 = (bf16[256,512]{1,0:T(8,128)(2,1)}, bf16[256,512]{1,0:T(8,128)(2,1)}, u32[]{:S(2)}, u32[]{:S(2)}) collective-permute-start(bf16[256,512]{1,0:T(8,128)(2,1)} %param.23), channel_id=1, source_target_pairs={{0,8},{4,12},{8,16},{12,20},{16,24},{20,28},{24,32},{28,36},{32,40... | collective-permute-start | bytes 786440 | tf_op jit(solution)/shard_map/ppermute | solution.py:36
  97.7 1.9 collective-permute-start.16
  102.1 3.6 %collective-permute-start.6 = (bf16[4,128,128]{2,1,0:T(8,128)(2,1)S(1)}, bf16[4,128,128]{2,1,0:T(8,128)(2,1)S(1)}, u32[]{:S(2)}, u32[]{:S(2)}) collective-permute-start(bf16[4,128,128]{2,1,0:T(8,128)(2,1)S(1)} %get-tuple-element.124), channel_id=1, source_target_pairs={{0,8},{4,12},{8,16},{12,20},{16,24},{20,28},{24,32},{28,36},{32,40... | collective-permute-start | bytes 393224 | tf_op jit(solution)/shard_map/ppermute | solution.py:36
  107.3 5.2 %collective-permute-done.6 = bf16[4,128,128]{2,1,0:T(8,128)(2,1)S(1)} collective-permute-done((bf16[4,128,128]{2,1,0:T(8,128)(2,1)S(1)}, bf16[4,128,128]{2,1,0:T(8,128)(2,1)S(1)}, u32[]{:S(2)}, u32[]{:S(2)}) %collective-permute-start.6) | collective-permute-done | bytes 131104 | tf_op jit(solution)/shard_map/ppermute | solution.py:36
  112.4 2.1 %collective-permute-start.1 = (bf16[4,128,128]{2,1,0:T(8,128)(2,1)S(1)}, bf16[4,128,128]{2,1,0:T(8,128)(2,1)S(1)}, u32[]{:S(2)}, u32[]{:S(2)}) collective-permute-start(bf16[4,128,128]{2,1,0:T(8,128)(2,1)S(1)} %get-tuple-element.126), channel_id=1, source_target_pairs={{0,8},{4,12},{8,16},{12,20},{16,24},{20,28},{24,32},{28,36},{32,40... | collective-permute-start | bytes 393224 | tf_op jit(solution)/shard_map/ppermute | solution.py:36
  116.2 5.2 %collective-permute-done.1 = bf16[4,128,128]{2,1,0:T(8,128)(2,1)S(1)} collective-permute-done((bf16[4,128,128]{2,1,0:T(8,128)(2,1)S(1)}, bf16[4,128,128]{2,1,0:T(8,128)(2,1)S(1)}, u32[]{:S(2)}, u32[]{:S(2)}) %collective-permute-start.1) | collective-permute-done | bytes 131104 | tf_op jit(solution)/shard_map/ppermute | solution.py:36
  121.4 1.9 collective-permute-start.7
  124.2 5.9 %collective-permute-start.2 = (bf16[4,128,128]{2,1,0:T(8,128)(2,1)}, bf16[4,128,128]{2,1,0:T(8,128)(2,1)}, u32[]{:S(2)}, u32[]{:S(2)}) collective-permute-start(bf16[4,128,128]{2,1,0:T(8,128)(2,1)} %get-tuple-element.130), channel_id=1, source_target_pairs={{0,16},{4,20},{8,24},{12,28},{16,32},{20,36},{24,40},{28,44},{32,4... | collective-permute-start | bytes 393224 | tf_op jit(solution)/shard_map/ppermute | solution.py:36
  130.1 1.8 copy.96
  131.9 2.4 %fusion.28 = f32[256,4,128]{0,2,1:T(8,128)} fusion(bf16[256,4,128]{0,2,1:T(8,128)(2,1)} %bitcast.320, f32[4,256,256]{1,2,0:T(8,128)} %copy-done.1, f32[4,256]{1,0:T(4,128)S(1)} %get-tuple-element.144, pred[256,256]{0,1:T(8,128)(4,1)} %copy-done.19, f32[256,4]{0,1:T(4,128)} %get-tuple-element.113), kind=kOutput, calls=%fused_computation.49 | convolution fusion | flops 68026368 | bytes 1908736 | tf_op jit(solution)/shard_map/hts,shd->htd/dot_general | solution.py:91
  134.3 1.8 copy.94
  136.1 2.4 %fusion.27 = f32[256,4,128]{0,2,1:T(8,128)} fusion(bf16[256,4,128]{0,2,1:T(8,128)(2,1)} %bitcast.321, f32[4,256,256]{1,2,0:T(8,128)} %copy-done.2, f32[4,256]{1,0:T(4,128)S(1)} %get-tuple-element.146, pred[256,256]{0,1:T(8,128)(4,1)S(1)} %get-tuple-element.120, f32[256,4]{0,1:T(4,128)} %get-tuple-element.112), kind=kOutput, calls=%fused_computation.48 | convolution fusion | flops 68026368 | bytes 1908736 | tf_op jit(solution)/shard_map/hts,shd->htd/dot_general | solution.py:91
  138.5 1.8 copy.92
  140.3 2.2 %fusion.26 = f32[256,4,128]{0,2,1:T(8,128)} fusion(bf16[256,4,128]{0,2,1:T(8,128)(2,1)} %bitcast.322, f32[4,256,256]{1,2,0:T(8,128)S(1)} %get-tuple-element.149, f32[4,256]{1,0:T(4,128)S(1)} %get-tuple-element.148, pred[256,256]{0,1:T(8,128)(4,1)S(1)} %get-tuple-element.122, f32[256,4]{0,1:T(4,128)} %get-tuple-element.111), kind=kOutput, calls=%fused_computation.47 | convolution fusion | flops 68026368 | bytes 1908736 | tf_op jit(solution)/shard_map/hts,shd->htd/dot_general | solution.py:91
  146.1 1.9 collective-permute-start.8
  149.3 1.9 collective-permute-start.3
  151.2 2.8 %collective-permute-done.8 = bf16[4,128,128]{2,1,0:T(8,128)(2,1)S(1)} collective-permute-done((bf16[4,128,128]{2,1,0:T(8,128)(2,1)S(1)}, bf16[4,128,128]{2,1,0:T(8,128)(2,1)S(1)}, u32[]{:S(2)}, u32[]{:S(2)}) %collective-permute-start.8) | collective-permute-done | bytes 131104 | tf_op jit(solution)/shard_map/ppermute | solution.py:36
  154.3 2.1 collective-permute-start.9
  157.3 1.9 collective-permute-start.4
  159.3 11.6 %collective-permute-done.9 = bf16[4,128,128]{2,1,0:T(8,128)(2,1)S(1)} collective-permute-done((bf16[4,128,128]{2,1,0:T(8,128)(2,1)S(1)}, bf16[4,128,128]{2,1,0:T(8,128)(2,1)S(1)}, u32[]{:S(2)}, u32[]{:S(2)}) %collective-permute-start.9) | collective-permute-done | bytes 131104 | tf_op jit(solution)/shard_map/ppermute | solution.py:36
  172.7 9.2 %collective-permute-done.10 = bf16[4,128,128]{2,1,0:T(8,128)(2,1)S(1)} collective-permute-done((bf16[4,128,128]{2,1,0:T(8,128)(2,1)S(1)}, bf16[4,128,128]{2,1,0:T(8,128)(2,1)S(1)}, u32[]{:S(2)}, u32[]{:S(2)}) %collective-permute-start.10) | collective-permute-done | bytes 131104 | tf_op jit(solution)/shard_map/ppermute | solution.py:36
  182.2 2.1 collective-permute-start.11
  184.7 6.0 %collective-permute-done.11 = bf16[4,128,128]{2,1,0:T(8,128)(2,1)S(1)} collective-permute-done((bf16[4,128,128]{2,1,0:T(8,128)(2,1)S(1)}, bf16[4,128,128]{2,1,0:T(8,128)(2,1)S(1)}, u32[]{:S(2)}, u32[]{:S(2)}) %collective-permute-start.11) | collective-permute-done | bytes 131104 | tf_op jit(solution)/shard_map/ppermute | solution.py:36
  194.4 15.0 %all_to_all.9 = bf16[4,64,2048]{2,1,0:T(8,128)(2,1)S(1)} all-to-all(bf16[4,64,2048]{2,1,0:T(8,128)(2,1)S(1)} %bitcast.318), channel_id=1, replica_groups=mesh['ctx'=64,'head'=4] {'head'}, dimensions={0} | all-to-all | bytes 2097152 | tf_op jit(solution)/shard_map/all_to_all | solution.py:210
  (199 shorter events, 52.8 us)
Async XLA Ops:
  0.0 192.1 %copy-start = (bf16[512,2048]{1,0:T(8,128)(2,1)S(1)}, bf16[512,2048]{1,0:T(8,128)(2,1)}, u32[]{:S(2)}) copy-start(bf16[512,2048]{1,0:T(8,128)(2,1)} %param.24) | copy-start | bytes 6291460
  0.0 15.3 %copy-start.37 = (f32[256,4]{0,1:T(4,128)S(1)}, f32[256,4]{0,1:T(4,128)}, u32[]{:S(2)}) copy-start(f32[256,4]{0,1:T(4,128)} %param.17) | copy-start | bytes 12292
  2.0 87.2 %collective-permute-start.15 = (bf16[256,512]{0,1:T(8,128)(2,1)}, bf16[256,512]{0,1:T(8,128)(2,1)}, u32[]{:S(2)}, u32[]{:S(2)}) collective-permute-start(bf16[256,512]{0,1:T(8,128)(2,1)} %copy.76), channel_id=1, source_target_pairs={{0,16},{4,20},{8,24},{12,28},{16,32},{20,36},{24,40},{28,44},{32,4... | collective-permute-start | bytes 786440 | tf_op jit(solution)/shard_map/ppermute | solution.py:36
  7.1 85.4 %collective-permute-start.13 = (bf16[256,512]{0,1:T(8,128)(2,1)}, bf16[256,512]{0,1:T(8,128)(2,1)}, u32[]{:S(2)}, u32[]{:S(2)}) collective-permute-start(bf16[256,512]{0,1:T(8,128)(2,1)} %copy.76), channel_id=1, source_target_pairs={{0,8},{4,12},{8,16},{12,20},{16,24},{20,28},{24,32},{28,36},{32,40... | collective-permute-start | bytes 786440 | tf_op jit(solution)/shard_map/ppermute | solution.py:36
  9.7 88.1 %collective-permute-start.14 = (bf16[256,512]{0,1:T(8,128)(2,1)}, bf16[256,512]{0,1:T(8,128)(2,1)}, u32[]{:S(2)}, u32[]{:S(2)}) collective-permute-start(bf16[256,512]{0,1:T(8,128)(2,1)} %copy.76), channel_id=1, source_target_pairs={{0,12},{4,16},{8,20},{12,24},{16,28},{20,32},{24,36},{28,40},{32,4... | collective-permute-start | bytes 786440 | tf_op jit(solution)/shard_map/ppermute | solution.py:36
  13.6 6.0 %copy-start.11 = (f32[4,64,4,128]{3,2,1,0:T(4,128)}, f32[4,64,4,128]{3,2,1,0:T(4,128)S(1)}, u32[]{:S(2)}) copy-start(f32[4,64,4,128]{3,2,1,0:T(4,128)S(1)} %reshape.511) | copy-start | bytes 1572868
  14.9 4.7 %copy-start.13 = (f32[4,64,4,128]{3,2,1,0:T(4,128)}, f32[4,64,4,128]{3,2,1,0:T(4,128)S(1)}, u32[]{:S(2)}) copy-start(f32[4,64,4,128]{3,2,1,0:T(4,128)S(1)} %reshape.512) | copy-start | bytes 1572868
  29.9 5.9 %copy-start.41 = (f32[4,4]{0,1:T(4,128)S(1)}, f32[4,4]{0,1:T(4,128)}, u32[]{:S(2)}) copy-start(f32[4,4]{0,1:T(4,128)} %exponential_bitcast_fusion) | copy-start | bytes 196
  40.1 25.4 %copy-start.32 = (f32[4,4,64]{2,1,0:T(4,128)S(1)}, f32[4,4,64]{2,1,0:T(4,128)}, u32[]{:S(2)}) copy-start(f32[4,4,64]{2,1,0:T(4,128)} %get-tuple-element.155) | copy-start | bytes 12292
  55.7 22.9 %collective-permute-start = (bf16[4,128,128]{2,1,0:T(8,128)(2,1)}, bf16[4,128,128]{2,1,0:T(8,128)(2,1)}, u32[]{:S(2)}, u32[]{:S(2)}) collective-permute-start(bf16[4,128,128]{2,1,0:T(8,128)(2,1)} %convert_element_type.112), channel_id=1, source_target_pairs={{0,4},{4,8},{8,12},{12,16},{16,20},{20,24},{24,28},{28,32},{32,36}... | collective-permute-start | bytes 393224 | tf_op jit(solution)/shard_map/ppermute | solution.py:36
  60.0 64.2 %collective-permute-start.19 = (bf16[256,512]{1,0:T(8,128)(2,1)}, bf16[256,512]{1,0:T(8,128)(2,1)}, u32[]{:S(2)}, u32[]{:S(2)}) collective-permute-start(bf16[256,512]{1,0:T(8,128)(2,1)} %param.23), channel_id=1, source_target_pairs={{0,16},{4,20},{8,24},{12,28},{16,32},{20,36},{24,40},{28,44},{32,4... | collective-permute-start | bytes 786440 | tf_op jit(solution)/shard_map/ppermute | solution.py:36
  69.5 5.6 %copy-start.8 = (f32[4,4,64,128]{3,2,1,0:T(8,128)S(1)}, f32[4,4,64,128]{3,2,1,0:T(8,128)}, u32[]{:S(2)}) copy-start(f32[4,4,64,128]{3,2,1,0:T(8,128)} %fusion.177) | copy-start | bytes 1572868
  71.7 5.9 %copy-start.3 = (bf16[256,512]{1,0:T(8,128)(2,1)S(1)}, bf16[256,512]{1,0:T(8,128)(2,1)}, u32[]{:S(2)}) copy-start(bf16[256,512]{1,0:T(8,128)(2,1)} %param.21) | copy-start | bytes 786436
  71.7 5.9 %copy-start.27 = (bf16[256,512]{1,0:T(8,128)(2,1)S(1)}, bf16[256,512]{1,0:T(8,128)(2,1)}, u32[]{:S(2)}) copy-start(bf16[256,512]{1,0:T(8,128)(2,1)} %param.22) | copy-start | bytes 786436
  77.6 28.9 %copy-start.20 = (pred[256,256]{0,1:T(8,128)(4,1)}, pred[256,256]{0,1:T(8,128)(4,1)S(1)}, u32[]{:S(2)}) copy-start(pred[256,256]{0,1:T(8,128)(4,1)S(1)} %get-tuple-element.123) | copy-start | bytes 196612
  77.6 28.9 %copy-start.22 = (pred[256,256]{0,1:T(8,128)(4,1)}, pred[256,256]{0,1:T(8,128)(4,1)S(1)}, u32[]{:S(2)}) copy-start(pred[256,256]{0,1:T(8,128)(4,1)S(1)} %get-tuple-element.119) | copy-start | bytes 196612
  77.6 29.5 %copy-start.19 = (pred[256,256]{0,1:T(8,128)(4,1)}, pred[256,256]{0,1:T(8,128)(4,1)S(1)}, u32[]{:S(2)}) copy-start(pred[256,256]{0,1:T(8,128)(4,1)S(1)} %get-tuple-element.121) | copy-start | bytes 196612
  77.9 28.6 %copy-start.6 = (f32[4,256,256]{1,2,0:T(8,128)}, f32[4,256,256]{1,2,0:T(8,128)S(1)}, u32[]{:S(2)}) copy-start(f32[4,256,256]{1,2,0:T(8,128)S(1)} %get-tuple-element.153) | copy-start | bytes 3145732
  77.9 37.6 %copy-start.29 = (f32[4,256]{1,0:T(4,128)}, f32[4,256]{1,0:T(4,128)S(1)}, u32[]{:S(2)}) copy-start(f32[4,256]{1,0:T(4,128)S(1)} %get-tuple-element.152) | copy-start | bytes 12292
  78.6 8.4 %collective-permute-start.5 = (bf16[4,128,128]{2,1,0:T(8,128)(2,1)S(1)}, bf16[4,128,128]{2,1,0:T(8,128)(2,1)S(1)}, u32[]{:S(2)}, u32[]{:S(2)}) collective-permute-start(bf16[4,128,128]{2,1,0:T(8,128)(2,1)S(1)} %copy-done.28), channel_id=1, source_target_pairs={{0,4},{4,8},{8,12},{12,16},{16,20},{20,24},{24,28},{28,32},{32,36}... | collective-permute-start | bytes 393224 | tf_op jit(solution)/shard_map/ppermute | solution.py:36
  87.0 15.1 %collective-permute-start.12 = (bf16[256,512]{0,1:T(8,128)(2,1)}, bf16[256,512]{0,1:T(8,128)(2,1)S(1)}, u32[]{:S(2)}, u32[]{:S(2)}) collective-permute-start(bf16[256,512]{0,1:T(8,128)(2,1)} %copy.76), channel_id=1, source_target_pairs={{0,4},{4,8},{8,12},{12,16},{16,20},{20,24},{24,28},{28,32},{32,36}... | collective-permute-start | bytes 786440 | tf_op jit(solution)/shard_map/ppermute | solution.py:36
  89.2 45.1 %collective-permute-start.18 = (bf16[256,512]{1,0:T(8,128)(2,1)}, bf16[256,512]{1,0:T(8,128)(2,1)}, u32[]{:S(2)}, u32[]{:S(2)}) collective-permute-start(bf16[256,512]{1,0:T(8,128)(2,1)} %param.23), channel_id=1, source_target_pairs={{0,12},{4,16},{8,20},{12,24},{16,28},{20,32},{24,36},{28,40},{32,4... | collective-permute-start | bytes 786440 | tf_op jit(solution)/shard_map/ppermute | solution.py:36
  92.4 14.6 %copy-start.1 = (f32[4,256,256]{1,2,0:T(8,128)}, f32[4,256,256]{1,2,0:T(8,128)S(1)}, u32[]{:S(2)}) copy-start(f32[4,256,256]{1,2,0:T(8,128)S(1)} %get-tuple-element.145) | copy-start | bytes 3145732
  92.4 46.0 %collective-permute-start.17 = (bf16[256,512]{1,0:T(8,128)(2,1)}, bf16[256,512]{1,0:T(8,128)(2,1)}, u32[]{:S(2)}, u32[]{:S(2)}) collective-permute-start(bf16[256,512]{1,0:T(8,128)(2,1)} %param.23), channel_id=1, source_target_pairs={{0,8},{4,12},{8,16},{12,20},{16,24},{20,28},{24,32},{28,36},{32,40... | collective-permute-start | bytes 786440 | tf_op jit(solution)/shard_map/ppermute | solution.py:36
  97.7 46.1 %collective-permute-start.16 = (bf16[256,512]{1,0:T(8,128)(2,1)}, bf16[256,512]{1,0:T(8,128)(2,1)}, u32[]{:S(2)}, u32[]{:S(2)}) collective-permute-start(bf16[256,512]{1,0:T(8,128)(2,1)} %param.23), channel_id=1, source_target_pairs={{0,4},{4,8},{8,12},{12,16},{16,20},{20,24},{24,28},{28,32},{32,36}... | collective-permute-start | bytes 786440 | tf_op jit(solution)/shard_map/ppermute | solution.py:36
  101.0 5.9 %copy-start.2 = (f32[4,256,256]{1,2,0:T(8,128)}, f32[4,256,256]{1,2,0:T(8,128)S(1)}, u32[]{:S(2)}) copy-start(f32[4,256,256]{1,2,0:T(8,128)S(1)} %get-tuple-element.147) | copy-start | bytes 3145732
  102.1 10.4 %collective-permute-start.6 = (bf16[4,128,128]{2,1,0:T(8,128)(2,1)S(1)}, bf16[4,128,128]{2,1,0:T(8,128)(2,1)S(1)}, u32[]{:S(2)}, u32[]{:S(2)}) collective-permute-start(bf16[4,128,128]{2,1,0:T(8,128)(2,1)S(1)} %get-tuple-element.124), channel_id=1, source_target_pairs={{0,8},{4,12},{8,16},{12,20},{16,24},{20,28},{24,32},{28,36},{32,40... | collective-permute-start | bytes 393224 | tf_op jit(solution)/shard_map/ppermute | solution.py:36
  112.4 9.0 %collective-permute-start.1 = (bf16[4,128,128]{2,1,0:T(8,128)(2,1)S(1)}, bf16[4,128,128]{2,1,0:T(8,128)(2,1)S(1)}, u32[]{:S(2)}, u32[]{:S(2)}) collective-permute-start(bf16[4,128,128]{2,1,0:T(8,128)(2,1)S(1)} %get-tuple-element.126), channel_id=1, source_target_pairs={{0,8},{4,12},{8,16},{12,20},{16,24},{20,28},{24,32},{28,36},{32,40... | collective-permute-start | bytes 393224 | tf_op jit(solution)/shard_map/ppermute | solution.py:36
  121.4 23.6 %collective-permute-start.7 = (bf16[4,128,128]{2,1,0:T(8,128)(2,1)}, bf16[4,128,128]{2,1,0:T(8,128)(2,1)}, u32[]{:S(2)}, u32[]{:S(2)}) collective-permute-start(bf16[4,128,128]{2,1,0:T(8,128)(2,1)} %get-tuple-element.128), channel_id=1, source_target_pairs={{0,16},{4,20},{8,24},{12,28},{16,32},{20,36},{24,40},{28,44},{32,4... | collective-permute-start | bytes 393224 | tf_op jit(solution)/shard_map/ppermute | solution.py:36
  124.2 23.9 %collective-permute-start.2 = (bf16[4,128,128]{2,1,0:T(8,128)(2,1)}, bf16[4,128,128]{2,1,0:T(8,128)(2,1)}, u32[]{:S(2)}, u32[]{:S(2)}) collective-permute-start(bf16[4,128,128]{2,1,0:T(8,128)(2,1)} %get-tuple-element.130), channel_id=1, source_target_pairs={{0,16},{4,20},{8,24},{12,28},{16,32},{20,36},{24,40},{28,44},{32,4... | collective-permute-start | bytes 393224 | tf_op jit(solution)/shard_map/ppermute | solution.py:36
  136.1 6.4 %copy-start.30 = (f32[4,256]{1,0:T(4,128)S(1)}, f32[4,256]{1,0:T(4,128)}, u32[]{:S(2)}) copy-start(f32[4,256]{1,0:T(4,128)} %copy-done.29) | copy-start | bytes 12292
  146.1 7.8 %collective-permute-start.8 = (bf16[4,128,128]{2,1,0:T(8,128)(2,1)S(1)}, bf16[4,128,128]{2,1,0:T(8,128)(2,1)S(1)}, u32[]{:S(2)}, u32[]{:S(2)}) collective-permute-start(bf16[4,128,128]{2,1,0:T(8,128)(2,1)S(1)} %get-tuple-element.132), channel_id=1, source_target_pairs={{0,32},{4,36},{8,40},{12,44},{16,48},{20,52},{24,56},{28,60},{32,6... | collective-permute-start | bytes 393224 | tf_op jit(solution)/shard_map/ppermute | solution.py:36
  149.3 7.8 %collective-permute-start.3 = (bf16[4,128,128]{2,1,0:T(8,128)(2,1)S(1)}, bf16[4,128,128]{2,1,0:T(8,128)(2,1)S(1)}, u32[]{:S(2)}, u32[]{:S(2)}) collective-permute-start(bf16[4,128,128]{2,1,0:T(8,128)(2,1)S(1)} %get-tuple-element.134), channel_id=1, source_target_pairs={{0,32},{4,36},{8,40},{12,44},{16,48},{20,52},{24,56},{28,60},{32,6... | collective-permute-start | bytes 393224 | tf_op jit(solution)/shard_map/ppermute | solution.py:36
  154.0 30.3 %copy-start.5 = (f32[4,256,256]{1,2,0:T(8,128)S(1)}, f32[4,256,256]{1,2,0:T(8,128)}, u32[]{:S(2)}) copy-start(f32[4,256,256]{1,2,0:T(8,128)} %copy-done.4) | copy-start | bytes 3145732
  154.0 30.3 %copy-start.21 = (pred[256,256]{0,1:T(8,128)(4,1)S(1)}, pred[256,256]{0,1:T(8,128)(4,1)}, u32[]{:S(2)}) copy-start(pred[256,256]{0,1:T(8,128)(4,1)} %copy-done.20) | copy-start | bytes 196612
  154.0 30.3 %copy-start.24 = (f32[256,4,128]{0,2,1:T(8,128)S(1)}, f32[256,4,128]{0,2,1:T(8,128)}, u32[]{:S(2)}) copy-start(f32[256,4,128]{0,2,1:T(8,128)} %fusion.28) | copy-start | bytes 1572868
  154.0 30.3 %copy-start.25 = (f32[256,4,128]{0,2,1:T(8,128)S(1)}, f32[256,4,128]{0,2,1:T(8,128)}, u32[]{:S(2)}) copy-start(f32[256,4,128]{0,2,1:T(8,128)} %fusion.27) | copy-start | bytes 1572868
  154.0 30.3 %copy-start.26 = (f32[256,4,128]{0,2,1:T(8,128)S(1)}, f32[256,4,128]{0,2,1:T(8,128)}, u32[]{:S(2)}) copy-start(f32[256,4,128]{0,2,1:T(8,128)} %fusion.26) | copy-start | bytes 1572868
  154.0 30.3 %copy-start.38 = (f32[256,4]{0,1:T(4,128)S(1)}, f32[256,4]{0,1:T(4,128)}, u32[]{:S(2)}) copy-start(f32[256,4]{0,1:T(4,128)} %get-tuple-element.108) | copy-start | bytes 12292
  154.0 30.3 %copy-start.39 = (f32[256,4]{0,1:T(4,128)S(1)}, f32[256,4]{0,1:T(4,128)}, u32[]{:S(2)}) copy-start(f32[256,4]{0,1:T(4,128)} %get-tuple-element.109) | copy-start | bytes 12292
  154.3 16.6 %collective-permute-start.9 = (bf16[4,128,128]{2,1,0:T(8,128)(2,1)S(1)}, bf16[4,128,128]{2,1,0:T(8,128)(2,1)S(1)}, u32[]{:S(2)}, u32[]{:S(2)}) collective-permute-start(bf16[4,128,128]{2,1,0:T(8,128)(2,1)S(1)} %get-tuple-element.136), channel_id=1, source_target_pairs={{0,64},{4,68},{8,72},{12,76},{16,80},{20,84},{24,88},{28,92},{32,9... | collective-permute-start | bytes 393224 | tf_op jit(solution)/shard_map/ppermute | solution.py:36
  157.3 15.1 %collective-permute-start.4 = (bf16[4,128,128]{2,1,0:T(8,128)(2,1)S(1)}, bf16[4,128,128]{2,1,0:T(8,128)(2,1)S(1)}, u32[]{:S(2)}, u32[]{:S(2)}) collective-permute-start(bf16[4,128,128]{2,1,0:T(8,128)(2,1)S(1)} %get-tuple-element.138), channel_id=1, source_target_pairs={{0,64},{4,68},{8,72},{12,76},{16,80},{20,84},{24,88},{28,92},{32,9... | collective-permute-start | bytes 393224 | tf_op jit(solution)/shard_map/ppermute | solution.py:36
  171.1 10.8 %collective-permute-start.10 = (bf16[4,128,128]{2,1,0:T(8,128)(2,1)S(1)}, bf16[4,128,128]{2,1,0:T(8,128)(2,1)S(1)}, u32[]{:S(2)}, u32[]{:S(2)}) collective-permute-start(bf16[4,128,128]{2,1,0:T(8,128)(2,1)S(1)} %get-tuple-element.140), channel_id=1, source_target_pairs={{0,128},{4,132},{8,136},{12,140},{16,144},{20,148},{24,152},{28,15... | collective-permute-start | bytes 393224 | tf_op jit(solution)/shard_map/ppermute | solution.py:36
  182.2 8.6 %copy-start.9 = (f32[4,4,64,128]{3,2,1,0:T(8,128)S(1)}, f32[4,4,64,128]{3,2,1,0:T(8,128)}, u32[]{:S(2)}) copy-start(f32[4,4,64,128]{3,2,1,0:T(8,128)} %convolution_add_fusion.2) | copy-start | bytes 1572868
  182.2 8.5 %copy-start.16 = (f32[4,4,64,128]{3,2,1,0:T(8,128)S(1)}, f32[4,4,64,128]{3,2,1,0:T(8,128)}, u32[]{:S(2)}) copy-start(f32[4,4,64,128]{3,2,1,0:T(8,128)} %fusion.37) | copy-start | bytes 1572868
  182.2 8.5 %collective-permute-start.11 = (bf16[4,128,128]{2,1,0:T(8,128)(2,1)S(1)}, bf16[4,128,128]{2,1,0:T(8,128)(2,1)S(1)}, u32[]{:S(2)}, u32[]{:S(2)}) collective-permute-start(bf16[4,128,128]{2,1,0:T(8,128)(2,1)S(1)} %fusion.36), channel_id=1, source_target_pairs={{0,4},{4,8},{8,12},{12,16},{16,20},{20,24},{24,28},{28,32},{32,36}... | collective-permute-start | bytes 393224 | tf_op jit(solution)/shard_map/ppermute | solution.py:36
  184.7 7.4 %copy-start.40 = (f32[512]{0:T(512)S(1)}, f32[512]{0:T(512)}, u32[]{:S(2)}) copy-start(f32[512]{0:T(512)} %broadcast_bitcast_fusion) | copy-start | bytes 6148
  184.7 7.4 %copy-start.43 = (bf16[256,512]{1,0:T(8,128)(2,1)S(1)}, bf16[256,512]{1,0:T(8,128)(2,1)}, u32[]{:S(2)}) copy-start(bf16[256,512]{1,0:T(8,128)(2,1)} %param.19) | copy-start | bytes 786436
  (18 other events, 56.9 us)

commit v2 on v1

--- a/solution.py
+++ b/solution.py
@@ -10,24 +10,41 @@
 highest = lax.Precision.HIGHEST
 
 
-def prefix_state(pair, axis):
+def prefix_state(pair, axis, fillers):
     place = lax.axis_index(axis)
     size = lax.axis_size(axis)
     mat, vec = pair
+    width = mat.shape[-1]
     distance = 1
+    done = []
+    pending = list(fillers)
+
+    def fill(far):
+        if not pending:
+            return far
+        work, inputs = pending.pop(0)
+        inputs, _ = lax.optimization_barrier((inputs, vec))
+        result, far = lax.optimization_barrier((work(*inputs), far))
+        done.append(result)
+        return far
+
     while distance < size:
         if 2 * distance >= size:
-            far_vec = passed_along(vec.astype(jnp.bfloat16), axis, distance).astype(jnp.float32)
+            far_vec = passed_along(vec.astype(jnp.bfloat16), axis, distance)
+            far_vec = fill(far_vec).astype(jnp.float32)
             vec = jnp.einsum("hij,hjk->hik", mat, far_vec, precision=highest) + vec
         else:
-            far_mat, far_vec = passed_along(
-                (mat.astype(jnp.bfloat16), vec.astype(jnp.bfloat16)), axis, distance
-            )
-            joined = chain_pairs((far_mat.astype(jnp.float32), far_vec.astype(jnp.float32)), (mat, vec))
-            mat = jnp.where(place >= distance, joined[0], mat)
-            vec = jnp.where(place >= distance, joined[1], vec)
+            packed = jnp.concatenate([mat, vec], axis=-1).astype(jnp.bfloat16)
+            far = fill(passed_along(packed, axis, distance)).astype(jnp.float32)
+            joined = jnp.einsum("hij,hjk->hik", mat, far, precision=highest)
+            mat = jnp.where(place >= distance, joined[..., :width], mat)
+            vec = joined[..., width:] + vec
         distance *= 2
-    return passed_along(vec.astype(jnp.bfloat16), axis, 1).astype(jnp.float32)
+    incoming = fill(passed_along(vec.astype(jnp.bfloat16), axis, 1)).astype(jnp.float32)
+    while pending:
+        work, inputs = pending.pop(0)
+        done.append(work(*inputs))
+    return incoming, done
 
 
 def passed_along(block, axis, distance):
@@ -72,10 +89,14 @@
         "...td,...te->...de", keys_end, writer, precision=highest
     )
     contrib = jnp.einsum("...td,...te->...de", keys_end, pseudo, precision=highest)
+    return (transition, contrib, (queries, keys_in, ratio_incl, decayed, pseudo, writer))
+
+
+def block_outputs(queries, keys_in, ratio_incl, decayed, pseudo, writer):
     mixing = ratio_incl * jnp.einsum("...td,...sd->...ts", queries, keys_in, precision=highest)
     local_out = jnp.matmul(mixing, pseudo, precision=highest)
     carry_out = decayed[..., None] * queries - jnp.matmul(mixing, writer, precision=highest)
-    return (transition, contrib, local_out, carry_out)
+    return (local_out, carry_out)
 
 
 def window_block(queries, keys_in, values_in, query_pos, key_pos):
@@ -130,26 +151,89 @@
     values_in = heads_blocks(delta_v)
     betas = beta.reshape(blocks, block_len, local_heads).transpose(2, 0, 1)
     log_rates = log_decay.reshape(blocks, block_len, local_heads).transpose(2, 0, 1)
-    transition, contrib, local_out, carry_out = block_terms(
-        queries, keys_in, values_in, betas, log_rates
-    )
+    transition, contrib, out_terms = block_terms(queries, keys_in, values_in, betas, log_rates)
     identity = jnp.broadcast_to(jnp.eye(DH, dtype=jnp.float32), (local_heads, DH, DH))
     zero_state = jnp.zeros((local_heads, DH, DH), jnp.float32)
-
-    def compose(carried, inputs):
-        after_pair = chain_pairs(carried, inputs)
-        return (after_pair, carried)
-
-    shard_pair, starts = lax.scan(
-        compose,
-        (identity, zero_state),
-        (transition.transpose(1, 0, 2, 3), contrib.transpose(1, 0, 2, 3)),
-    )
-    start_mats = starts[0].transpose(1, 0, 2, 3)
-    start_vecs = starts[1].transpose(1, 0, 2, 3)
-    own_out = local_out + jnp.einsum("hntd,hnde->hnte", carry_out, start_vecs, precision=highest)
-    reach = jnp.einsum("hntd,hnde->hnte", carry_out, start_mats, precision=highest)
-    incoming_state = prefix_state(shard_pair, "ctx")
+    start_mats = [identity]
+    start_vecs = [zero_state]
+    run_mat, run_vec = transition[:, 0], contrib[:, 0]
+    for block in range(1, blocks):
+        start_mats.append(run_mat)
+        start_vecs.append(run_vec)
+        joined = jnp.einsum(
+            "hij,hjk->hik",
+            transition[:, block],
+            jnp.concatenate([run_mat, run_vec], axis=-1),
+            precision=highest,
+        )
+        run_mat = joined[..., :DH]
+        run_vec = joined[..., DH:] + contrib[:, block]
+    start_mats = jnp.stack(start_mats, axis=1)
+    start_vecs = jnp.stack(start_vecs, axis=1)
+    shard_pair = (run_mat, run_vec)
+    position = lax.axis_index("ctx")
+    spans = WINDOW // rows_here
+    far_blocks = [
+        passed_along(jnp.concatenate([attn_k, attn_v], axis=-1), "ctx", back)
+        for back in range(1, spans + 1)
+    ]
+    shard_pair, far_blocks = lax.optimization_barrier((shard_pair, far_blocks))
+
+    def delta_local(out_terms, start_mats, start_vecs):
+        local_out, carry_out = block_outputs(*out_terms)
+        own_out = local_out + jnp.einsum(
+            "hntd,hnde->hnte", carry_out, start_vecs, precision=highest
+        )
+        reach = jnp.einsum("hntd,hnde->hnte", carry_out, start_mats, precision=highest)
+        return own_out, reach
+
+    query_rows = attn_q.reshape(rows_here, local_heads, DH)
+    query_pos = position * rows_here + jnp.arange(rows_here, dtype=jnp.int32)
+    key_width = attn_k.shape[1]
+
+    def attend(query_rows, key_rows, value_rows, back):
+        key_pos = query_pos - back * rows_here
+        return window_block(
+            query_rows,
+            key_rows.reshape(rows_here, local_heads, DH),
+            value_rows.reshape(rows_here, local_heads, DH),
+            query_pos,
+            key_pos,
+        )
+
+    def far_attend(query_rows, block, back):
+        return attend(query_rows, block[:, :key_width], block[:, key_width:], back)
+
+    def combine(w_attn_out, *parts):
+        maxima = [part[0] for part in parts]
+        top = maxima[0]
+        for block_max in maxima[1:]:
+            top = jnp.maximum(top, block_max)
+        numer = jnp.zeros_like(parts[0][1])
+        denom = jnp.zeros_like(parts[0][2])
+        for block_max, block_num, block_den in parts:
+            factor = jnp.exp(block_max - top)
+            numer = numer + factor[..., None] * block_num
+            denom = denom + factor * block_den
+        attn_heads = (
+            (numer / denom[..., None])
+            .transpose(1, 0, 2)
+            .reshape(rows_here, local_heads * DH)
+            .astype(jnp.bfloat16)
+        )
+        return jnp.dot(attn_heads, w_attn_out, preferred_element_type=jnp.float32)
+
+    fillers = [
+        (delta_local, (out_terms, start_mats, start_vecs)),
+        (lambda q, k, v: attend(q, k, v, 0), (query_rows, attn_k, attn_v)),
+    ]
+    for back in range(1, spans + 1):
+        fillers.append(
+            (lambda q, blk, back=back: far_attend(q, blk, back), (query_rows, far_blocks[back - 1]))
+        )
+    incoming_state, results = prefix_state(shard_pair, "ctx", fillers)
+    (own_out, reach), attn_parts = results[0], results[1:]
+    attn_sum = combine(w_attn_out, *attn_parts)
     delta_raw = own_out + jnp.einsum("hntd,hde->hnte", reach, incoming_state, precision=highest)
     delta_raw = delta_raw.transpose(1, 2, 0, 3).reshape(rows_here, local_heads, DH)
     gate_act = jax.nn.silu(out_gate.astype(jnp.float32).reshape(rows_here, local_heads, DH))
@@ -160,51 +244,8 @@
         * gate_act
     )
     delta_heads = normed.reshape(rows_here, local_heads * DH).astype(jnp.bfloat16)
-    position = lax.axis_index("ctx")
-    query_rows = attn_q.reshape(rows_here, local_heads, DH)
-    query_pos = position * rows_here + jnp.arange(rows_here, dtype=jnp.int32)
-    maxima, numers, denoms = ([], [], [])
-    own_max, own_num, own_den = window_block(
-        query_rows,
-        attn_k.reshape(rows_here, local_heads, DH),
-        attn_v.reshape(rows_here, local_heads, DH),
-        query_pos,
-        query_pos,
-    )
-    maxima.append(own_max)
-    numers.append(own_num)
-    denoms.append(own_den)
-    for back in range(1, WINDOW // rows_here + 1):
-        keys_far, values_far = passed_along((attn_k, attn_v), "ctx", back)
-        key_pos = (position - back) * rows_here + jnp.arange(rows_here, dtype=jnp.int32)
-        remote_maximum, far_num, far_den = window_block(
-            query_rows,
-            keys_far.reshape(rows_here, local_heads, DH),
-            values_far.reshape(rows_here, local_heads, DH),
-            query_pos,
-            key_pos,
-        )
-        maxima.append(remote_maximum)
-        numers.append(far_num)
-        denoms.append(far_den)
-    top = maxima[0]
-    for block_max in maxima[1:]:
-        top = jnp.maximum(top, block_max)
-    numer = jnp.zeros_like(numers[0])
-    denom = jnp.zeros_like(denoms[0])
-    for block_max, block_num, block_den in zip(maxima, numers, denoms):
-        factor = jnp.exp(block_max - top)
-        numer = numer + factor[..., None] * block_num
-        denom = denom + factor * block_den
-    attn_heads = (
-        (numer / denom[..., None])
-        .transpose(1, 0, 2)
-        .reshape(rows_here, local_heads * DH)
-        .astype(jnp.bfloat16)
-    )
-    running_partial_sum = jnp.dot(delta_heads, w_delta_out, preferred_element_type=jnp.float32)
-    running_partial_sum = running_partial_sum + jnp.dot(
-        attn_heads, w_attn_out, preferred_element_type=jnp.float32
+    running_partial_sum = attn_sum + jnp.dot(
+        delta_heads, w_delta_out, preferred_element_type=jnp.float32
     )
     n_head = lax.axis_size("head")
     pieces = lax.all_to_all(

time: 212 us -> 170 us (0.80)
  matrix products: 63.7 us -> 34.6 us
  starting transfers between devices: 54.1 us -> 35 us
  other arithmetic: 10.6 us -> 19.4 us
  waiting for transfers between devices: 46.8 us -> 44.4 us
    ppermute x20 -> x11, starting transfers between devices: 54.1 us -> 35 us  [passed_along(): return lax.ppermute(block, axis, route)]
    dot_general x24 -> x14, matrix products: 29.3 us -> 12.2 us  [the longest x1 2.13 us: delta_local(): jnp.einsum('hntd,hnde->hnte', carry_out, start_vecs, precision=highest)]
    dot_general x5, matrix products: 8.65 us -> 2 us  [window_block(): jnp.einsum('hts,shd->htd', probs, values_in, preferred_element_type=jnp.f...]
    ppermute x4 -> x0, local copies, waits for them, and re-layouts: 6.47 us -> none  [passed_along(): return lax.ppermute(block, axis, route)]
    another operation x2 -> x10, other arithmetic: 0.01 us -> 5.32 us  [the longest x3 3.65 us: shards(): start_mats = jnp.stack(start_mats, axis=1)]
    slice x0 -> x5, local copies, waits for them, and re-layouts: none -> 5.02 us  [the longest x4 4.26 us: far_attend(): return attend(query_rows, block[:, :key_width], block[:, key_width:], back)]
    dynamic_update_slice x4 -> x0, other arithmetic: 3.43 us -> none  [shards(): lax.scan(compose, (identity, zero_state), (transition.transpose(1, 0, 2,...]
    dot_general x5, matrix products: 4.65 us -> 1.84 us  [window_block(): jnp.einsum('thd,shd->hts', queries, keys_in, preferred_element_type=jnp.f...]
  transfers between devices with their start and end apart: 20 -> 11, of which waited for: 9 -> 7; matrix products, arithmetic and copies ran while one was open for 41% -> 34% of each run, Pallas kernels for 0% -> 0%
where the time goes in v2:
time: 170 us; the launch traced here: 169 us
  waiting for transfers between devices  44.4 us (26%)
  starting transfers between devices  35 us (21%)
  matrix products  34.6 us (20%)
  other arithmetic  19.4 us (11%)
  local copies, waits for them, and re-layouts  17.8 us (10%)
  blocking collectives  17 us (10%)
    ppermute x11, waiting for transfers between devices, passed_along(): return lax.ppermute(block, axis, route)  44.4 us
    ppermute x11, starting transfers between devices, passed_along(): return lax.ppermute(block, axis, route)  35 us
    all_to_all x1, blocking collectives, shards(): lax.all_to_all(running_partial_sum.astype(jnp.bfloat16), 'head', 0, 0, ti...  17 us
    unnamed x53, local copies, waits for them, and re-layouts  4.92 us
    slice x4, local copies, waits for them, and re-layouts, far_attend(): return attend(query_rows, block[:, :key_width], block[:, key_width:], back)  4.26 us
    another operation x3, other arithmetic, shards(): start_mats = jnp.stack(start_mats, axis=1)  3.65 us
  transfers between devices with their start and end apart: 11, of which 7 were waited for; matrix products, arithmetic and copies ran while one was open for 34% of the time, Pallas kernels for 0%

profile of v2, /device:TPU:160, one launch (start us, length us, event | category | flops | bytes accessed | tf_op | source)
XLA Modules:
  0.0 169.2 jit_solution(13961567179904559327)
XLA Ops:
  0.0 1.2 copy.149
  1.3 1.1 copy.150
  3.2 1.9 %collective-permute-start = (bf16[256,1024]{0,1:T(8,128)(2,1)}, bf16[256,1024]{0,1:T(8,128)(2,1)}, u32[]{:S(2)}, u32[]{:S(2)}) collective-permute-start(bf16[256,1024]{0,1:T(8,128)(2,1)} %pad_maximum_fusion.2), channel_id=1, source_target_pairs={{0,4},{4,8},{8,12},{12,16},{16,20},{20,24},{24,28},{28,32},{32,36}... | collective-permute-start | bytes 1572872 | tf_op jit(solution)/shard_map/ppermute | solution.py:53
  5.1 3.5 %collective-permute-start.1 = (bf16[256,1024]{0,1:T(8,128)(2,1)}, bf16[256,1024]{0,1:T(8,128)(2,1)}, u32[]{:S(2)}, u32[]{:S(2)}) collective-permute-start(bf16[256,1024]{0,1:T(8,128)(2,1)} %pad_maximum_fusion.2), channel_id=1, source_target_pairs={{0,8},{4,12},{8,16},{12,20},{16,24},{20,28},{24,32},{28,36},{32,40... | collective-permute-start | bytes 1572872 | tf_op jit(solution)/shard_map/ppermute | solution.py:53
  8.6 4.2 %collective-permute-start.2 = (bf16[256,1024]{0,1:T(8,128)(2,1)}, bf16[256,1024]{0,1:T(8,128)(2,1)}, u32[]{:S(2)}, u32[]{:S(2)}) collective-permute-start(bf16[256,1024]{0,1:T(8,128)(2,1)} %pad_maximum_fusion.2), channel_id=1, source_target_pairs={{0,12},{4,16},{8,20},{12,24},{16,28},{20,32},{24,36},{28,40},{32,4... | collective-permute-start | bytes 1572872 | tf_op jit(solution)/shard_map/ppermute | solution.py:53
  12.8 4.2 %collective-permute-start.3 = (bf16[256,1024]{0,1:T(8,128)(2,1)}, bf16[256,1024]{0,1:T(8,128)(2,1)}, u32[]{:S(2)}, u32[]{:S(2)}) collective-permute-start(bf16[256,1024]{0,1:T(8,128)(2,1)} %pad_maximum_fusion.2), channel_id=1, source_target_pairs={{0,16},{4,20},{8,24},{12,28},{16,32},{20,36},{24,40},{28,44},{32,4... | collective-permute-start | bytes 1572872 | tf_op jit(solution)/shard_map/ppermute | solution.py:53
  21.4 0.9 reduce_window_sum.11
  22.6 1.0 fusion.6
  31.6 2.1 %convolution_subtract_fusion = f32[4,4,128,128]{2,3,1,0:T(8,128)S(1)} fusion(f32[4,4,64,128]{3,2,1,0:T(8,128)S(1)} %fusion.66, f32[128,128]{0,1:T(8,128)S(1)} %fusion.123, f32[4,4]{1,0:T(4,128)S(1)} %exp.58, f32[4,4,64,128]{3,2,1,0:T(8,128)S(1)} %bitcast_divide_fusion.2, f32[4,4,64]{2,1,0:T(4,128)S(1)} %get-tuple-element.157), kind=kOutput, calls=%fused_computation.2 | convolution fusion | flops 201981952 | bytes 2166848 | tf_op jit(solution)/shard_map/...td,...te->...de/dot_general | solution.py:88
  33.7 1.0 copy-done.5
  35.4 1.9 %reshape.419 = f32[4,64,4,128]{3,2,1,0:T(4,128)} reshape(bf16[256,512]{1,0:T(8,128)(2,1)} %param.14) | data formatting | bytes 786432 | tf_op jit(solution)/shard_map/transpose | solution.py:146
  37.3 1.8 %fusion.53 = f32[4,4,64,128]{3,2,1,0:T(8,128)S(1)} fusion(f32[4,4,64,64]{3,2,1,0:T(8,128)S(1)} %fusion.163, f32[4,64,4,128]{3,2,1,0:T(4,128)} %reshape.419, f32[4,4,64]{2,1,0:T(4,128)S(1)} %bitcast.188), kind=kOutput, calls=%fused_computation.77 | convolution fusion | flops 100794368 | bytes 1314816 | tf_op jit(solution)/shard_map/dot_general | solution.py:83
  39.2 2.2 %fusion.83 = f32[4,4,128,128]{2,3,1,0:T(8,128)S(1)} fusion(f32[4,4,64,128]{3,2,1,0:T(8,128)S(1)} %fusion.53, f32[4,4,64,128]{3,2,1,0:T(8,128)S(1)} %bitcast_divide_fusion.2, f32[4,4,64]{2,1,0:T(4,128)S(1)} %get-tuple-element.157), kind=kOutput, calls=%fused_computation.112 | convolution fusion | flops 201457664 | bytes 2101248 | tf_op jit(solution)/shard_map/...td,...te->...de/dot_general | solution.py:91
  46.3 1.0 fusion.27
  47.3 1.1 reshape.420
  49.3 2.0 %fusion.118 = (pred[256,256]{0,1:T(8,128)(4,1)S(1)}, pred[256,256]{0,1:T(8,128)(4,1)}, pred[256,256]{0,1:T(8,128)(4,1)S(1)}, pred[256,256]{0,1:T(8,128)(4,1)}, pred[256,256]{0,1:T(8,128)(4,1)}) fusion(s32[256]{0:T(256)} %get-tuple-element.174, s32[256]{0:T(256)} %get-tuple-element.173, pred[256]{0:T(512)(128)(4,1)} %get-tuple-element.178, ...), kind=kLoop, calls=%fused_computation.177 | loop fusion | flops 1638400 | bytes 334080 | tf_op jit(solution)/shard_map/and | solution.py:107
  51.3 0.9 stack_broadcast_in_dim.6
  52.1 2.1 %pad_maximum_fusion = f32[4,4,128,128]{2,3,1,0:T(8,128)} fusion(f32[4,1,128,128]{2,3,1,0:T(8,128)} %get-tuple-element.150, f32[4,1,128,128]{2,3,1,0:T(8,128)} %get-tuple-element.147, f32[4,1,128,128]{2,3,1,0:T(8,128)S(1)} %copy-done.13, f32[4,1,128,128]{2,3,1,0:T(8,128)S(1)} %stack_broadcast_in_dim.6), kind=kLoop, calls=%fused_computation.21 | loop fusion | flops 786432 | bytes 2097152 | tf_op jit(solution)/shard_map/stack | solution.py:171
  54.2 1.0 reshape.401
  55.3 1.3 pad_maximum_fusion.1
  57.0 2.1 %collective-permute-start.4 = (bf16[4,128,256]{1,2,0:T(8,128)(2,1)S(1)}, bf16[4,128,256]{1,2,0:T(8,128)(2,1)S(1)}, u32[]{:S(2)}, u32[]{:S(2)}) collective-permute-start(bf16[4,128,256]{1,2,0:T(8,128)(2,1)S(1)} %pad_maximum_fusion.3), channel_id=1, source_target_pairs={{0,4},{4,8},{8,12},{12,16},{16,20},{20,24},{24,28},{28,32},{32,36}... | collective-permute-start | bytes 786440 | tf_op jit(solution)/shard_map/ppermute | solution.py:53
  59.1 0.9 convolution_multiply_fusion.5
  61.4 2.1 %convolution_add_fusion.1 = f32[4,4,64,128]{3,2,1,0:T(8,128)S(1)} fusion(f32[4,4,64,128]{3,2,1,0:T(8,128)S(1)} %fusion.164, f32[4,4,64,128]{3,2,1,0:T(8,128)S(1)} %convolution_subtract_fusion.1, f32[4,4,128,128]{2,3,0,1:T(8,128)S(1)} %pad_maximum_fusion.1), kind=kOutput, calls=%fused_computation.13 | convolution fusion | flops 201457664 | bytes 2621440 | tf_op jit(solution)/shard_map/hntd,hnde->hnte/dot_general | solution.py:184
  63.6 2.1 %fusion.165 = f32[4,4,64,128]{3,2,1,0:T(8,128)S(1)} fusion(f32[4,4,64,128]{3,2,1,0:T(8,128)S(1)} %convolution_subtract_fusion.1, f32[4,4,128,128]{2,3,1,0:T(8,128)S(1)} %copy-done.7), kind=kOutput, calls=%fused_computation.252 | convolution fusion | flops 201326592 | bytes 2097152 | tf_op jit(solution)/shard_map/hntd,hnde->hnte/dot_general | solution.py:187
  65.7 5.8 %collective-permute-done.4 = bf16[4,128,256]{1,2,0:T(8,128)(2,1)S(1)} collective-permute-done((bf16[4,128,256]{1,2,0:T(8,128)(2,1)S(1)}, bf16[4,128,256]{1,2,0:T(8,128)(2,1)S(1)}, u32[]{:S(2)}, u32[]{:S(2)}) %collective-permute-start.4) | collective-permute-done | bytes 262176 | tf_op jit(solution)/shard_map/ppermute | solution.py:53
  72.1 6.0 %collective-permute-start.5 = (bf16[4,128,256]{1,2,0:T(8,128)(2,1)S(1)}, bf16[4,128,256]{1,2,0:T(8,128)(2,1)S(1)}, u32[]{:S(2)}, u32[]{:S(2)}) collective-permute-start(bf16[4,128,256]{1,2,0:T(8,128)(2,1)S(1)} %pad_maximum_fusion.4), channel_id=1, source_target_pairs={{0,8},{4,12},{8,16},{12,20},{16,24},{20,28},{24,32},{28,36},{32,40... | collective-permute-start | bytes 786440 | tf_op jit(solution)/shard_map/ppermute | solution.py:53
  79.1 6.1 %collective-permute-done.5 = bf16[4,128,256]{1,2,0:T(8,128)(2,1)S(1)} collective-permute-done((bf16[4,128,256]{1,2,0:T(8,128)(2,1)S(1)}, bf16[4,128,256]{1,2,0:T(8,128)(2,1)S(1)}, u32[]{:S(2)}, u32[]{:S(2)}) %collective-permute-start.5) | collective-permute-done | bytes 262176 | tf_op jit(solution)/shard_map/ppermute | solution.py:53
  85.7 3.6 %collective-permute-start.6 = (bf16[4,128,256]{1,2,0:T(8,128)(2,1)S(1)}, bf16[4,128,256]{1,2,0:T(8,128)(2,1)S(1)}, u32[]{:S(2)}, u32[]{:S(2)}) collective-permute-start(bf16[4,128,256]{1,2,0:T(8,128)(2,1)S(1)} %pad_maximum_fusion.5), channel_id=1, source_target_pairs={{0,16},{4,20},{8,24},{12,28},{16,32},{20,36},{24,40},{28,44},{32,4... | collective-permute-start | bytes 786440 | tf_op jit(solution)/shard_map/ppermute | solution.py:53
  89.3 1.1 fusion.152
  91.3 6.9 %collective-permute-done.6 = bf16[4,128,256]{1,2,0:T(8,128)(2,1)S(1)} collective-permute-done((bf16[4,128,256]{1,2,0:T(8,128)(2,1)S(1)}, bf16[4,128,256]{1,2,0:T(8,128)(2,1)S(1)}, u32[]{:S(2)}, u32[]{:S(2)}) %collective-permute-start.6) | collective-permute-done | bytes 262176 | tf_op jit(solution)/shard_map/ppermute | solution.py:53
  98.8 2.9 %collective-permute-start.7 = (bf16[4,128,256]{1,2,0:T(8,128)(2,1)S(1)}, bf16[4,128,256]{1,2,0:T(8,128)(2,1)S(1)}, u32[]{:S(2)}, u32[]{:S(2)}) collective-permute-start(bf16[4,128,256]{1,2,0:T(8,128)(2,1)S(1)} %pad_maximum_fusion.6), channel_id=1, source_target_pairs={{0,32},{4,36},{8,40},{12,44},{16,48},{20,52},{24,56},{28,60},{32,6... | collective-permute-start | bytes 786440 | tf_op jit(solution)/shard_map/ppermute | solution.py:53
  101.7 1.1 fusion.151
  103.8 4.4 %collective-permute-done.7 = bf16[4,128,256]{1,2,0:T(8,128)(2,1)S(1)} collective-permute-done((bf16[4,128,256]{1,2,0:T(8,128)(2,1)S(1)}, bf16[4,128,256]{1,2,0:T(8,128)(2,1)S(1)}, u32[]{:S(2)}, u32[]{:S(2)}) %collective-permute-start.7) | collective-permute-done | bytes 262176 | tf_op jit(solution)/shard_map/ppermute | solution.py:53
  108.6 3.4 %collective-permute-start.8 = (bf16[4,128,256]{1,2,0:T(8,128)(2,1)S(1)}, bf16[4,128,256]{1,2,0:T(8,128)(2,1)S(1)}, u32[]{:S(2)}, u32[]{:S(2)}) collective-permute-start(bf16[4,128,256]{1,2,0:T(8,128)(2,1)S(1)} %pad_maximum_fusion.7), channel_id=1, source_target_pairs={{0,64},{4,68},{8,72},{12,76},{16,80},{20,84},{24,88},{28,92},{32,9... | collective-permute-start | bytes 786440 | tf_op jit(solution)/shard_map/ppermute | solution.py:53
  112.0 1.1 fusion.150
  114.1 8.5 %collective-permute-done.8 = bf16[4,128,256]{1,2,0:T(8,128)(2,1)S(1)} collective-permute-done((bf16[4,128,256]{1,2,0:T(8,128)(2,1)S(1)}, bf16[4,128,256]{1,2,0:T(8,128)(2,1)S(1)}, u32[]{:S(2)}, u32[]{:S(2)}) %collective-permute-start.8) | collective-permute-done | bytes 262176 | tf_op jit(solution)/shard_map/ppermute | solution.py:53
  123.0 1.1 fusion.149
  124.0 1.3 collective-permute-start.9
  126.3 10.8 %collective-permute-done.9 = bf16[4,128,128]{1,2,0:T(8,128)(2,1)S(1)} collective-permute-done((bf16[4,128,128]{1,2,0:T(8,128)(2,1)S(1)}, bf16[4,128,128]{1,2,0:T(8,128)(2,1)S(1)}, u32[]{:S(2)}, u32[]{:S(2)}) %collective-permute-start.9) | collective-permute-done | bytes 131104 | tf_op jit(solution)/shard_map/ppermute | solution.py:53
  137.2 0.9 fusion.7
  138.1 1.9 %collective-permute-start.10 = (bf16[4,128,128]{1,2,0:T(8,128)(2,1)}, bf16[4,128,128]{1,2,0:T(8,128)(2,1)S(1)}, u32[]{:S(2)}, u32[]{:S(2)}) collective-permute-start(bf16[4,128,128]{1,2,0:T(8,128)(2,1)} %fusion.7), channel_id=1, source_target_pairs={{0,4},{4,8},{8,12},{12,16},{16,20},{20,24},{24,28},{28,32},{32,36}... | collective-permute-start | bytes 393224 | tf_op jit(solution)/shard_map/ppermute | solution.py:53
  140.0 1.6 fusion.119
  141.7 1.1 copy.194
  142.8 2.1 %fusion.171 = f32[256,2048]{1,0:T(8,128)} fusion(bf16[256,512]{0,1:T(8,128)(2,1)S(1)} %bitcast.174, bf16[512,2048]{1,0:T(8,128)(2,1)S(1)} %copy-done), kind=kOutput, calls=%fused_computation.258 | convolution fusion | flops 536870912 | bytes 4456448 | tf_op jit(solution)/shard_map/dot_general | solution.py:224
  144.9 1.8 %collective-permute-done.10 = bf16[4,128,128]{1,2,0:T(8,128)(2,1)S(1)} collective-permute-done((bf16[4,128,128]{1,2,0:T(8,128)(2,1)}, bf16[4,128,128]{1,2,0:T(8,128)(2,1)S(1)}, u32[]{:S(2)}, u32[]{:S(2)}) %collective-permute-start.10) | collective-permute-done | bytes 131104 | tf_op jit(solution)/shard_map/ppermute | solution.py:53
  148.1 3.1 %fusion = bf16[256,2048]{1,0:T(8,128)(2,1)S(1)} fusion(f32[256,2048]{1,0:T(8,128)} %fusion.171, bf16[512,2048]{1,0:T(8,128)(2,1)} %param.22, bf16[256,512]{1,0:T(8,128)(2,1)} %param.17, f32[32,8,4,128]{3,2,1,0:T(4,128)S(1)} %bitcast.184, f32[32,8,4,128]{3,2,1,0:T(4,128)S(1)} %bitcast.186, f32[512]{0:T(512)S(1)} %copy-done.23), kind=kOutput, calls=%fused_computation.1 | convolution fusion | flops 539099136 | bytes 6555648 | tf_op jit(solution)/shard_map/dot_general | solution.py:247
  151.3 17.0 %all_to_all.9 = bf16[4,64,2048]{2,1,0:T(8,128)(2,1)S(1)} all-to-all(bf16[4,64,2048]{2,1,0:T(8,128)(2,1)S(1)} %bitcast.175), channel_id=1, replica_groups=mesh['ctx'=64,'head'=4] {'head'}, dimensions={0} | all-to-all | bytes 2097152 | tf_op jit(solution)/shard_map/all_to_all | solution.py:251
  168.2 0.9 reduce_sum.92
  (138 shorter events, 30.0 us)
Async XLA Ops:
  0.0 142.8 %copy-start = (bf16[512,2048]{1,0:T(8,128)(2,1)S(1)}, bf16[512,2048]{1,0:T(8,128)(2,1)}, u32[]{:S(2)}) copy-start(bf16[512,2048]{1,0:T(8,128)(2,1)} %param.23) | copy-start | bytes 6291460
  0.0 20.6 %copy-start.19 = (bf16[256,512]{1,0:T(8,128)(2,1)S(1)}, bf16[256,512]{1,0:T(8,128)(2,1)}, u32[]{:S(2)}) copy-start(bf16[256,512]{1,0:T(8,128)(2,1)} %param.13) | copy-start | bytes 786436
  1.2 20.0 %copy-start.21 = (f32[256,4]{0,1:T(4,128)S(1)}, f32[256,4]{0,1:T(4,128)}, u32[]{:S(2)}) copy-start(f32[256,4]{0,1:T(4,128)} %param.16) | copy-start | bytes 12292
  1.3 20.0 %copy-start.22 = (f32[256,4]{0,1:T(4,128)S(1)}, f32[256,4]{0,1:T(4,128)}, u32[]{:S(2)}) copy-start(f32[256,4]{0,1:T(4,128)} %param.15) | copy-start | bytes 12292
  3.2 53.7 %collective-permute-start = (bf16[256,1024]{0,1:T(8,128)(2,1)}, bf16[256,1024]{0,1:T(8,128)(2,1)}, u32[]{:S(2)}, u32[]{:S(2)}) collective-permute-start(bf16[256,1024]{0,1:T(8,128)(2,1)} %pad_maximum_fusion.2), channel_id=1, source_target_pairs={{0,4},{4,8},{8,12},{12,16},{16,20},{20,24},{24,28},{28,32},{32,36}... | collective-permute-start | bytes 1572872 | tf_op jit(solution)/shard_map/ppermute | solution.py:53
  5.1 51.8 %collective-permute-start.1 = (bf16[256,1024]{0,1:T(8,128)(2,1)}, bf16[256,1024]{0,1:T(8,128)(2,1)}, u32[]{:S(2)}, u32[]{:S(2)}) collective-permute-start(bf16[256,1024]{0,1:T(8,128)(2,1)} %pad_maximum_fusion.2), channel_id=1, source_target_pairs={{0,8},{4,12},{8,16},{12,20},{16,24},{20,28},{24,32},{28,36},{32,40... | collective-permute-start | bytes 1572872 | tf_op jit(solution)/shard_map/ppermute | solution.py:53
  8.6 48.3 %collective-permute-start.2 = (bf16[256,1024]{0,1:T(8,128)(2,1)}, bf16[256,1024]{0,1:T(8,128)(2,1)}, u32[]{:S(2)}, u32[]{:S(2)}) collective-permute-start(bf16[256,1024]{0,1:T(8,128)(2,1)} %pad_maximum_fusion.2), channel_id=1, source_target_pairs={{0,12},{4,16},{8,20},{12,24},{16,28},{20,32},{24,36},{28,40},{32,4... | collective-permute-start | bytes 1572872 | tf_op jit(solution)/shard_map/ppermute | solution.py:53
  12.8 44.1 %collective-permute-start.3 = (bf16[256,1024]{0,1:T(8,128)(2,1)}, bf16[256,1024]{0,1:T(8,128)(2,1)}, u32[]{:S(2)}, u32[]{:S(2)}) collective-permute-start(bf16[256,1024]{0,1:T(8,128)(2,1)} %pad_maximum_fusion.2), channel_id=1, source_target_pairs={{0,16},{4,20},{8,24},{12,28},{16,32},{20,36},{24,40},{28,44},{32,4... | collective-permute-start | bytes 1572872 | tf_op jit(solution)/shard_map/ppermute | solution.py:53
  17.1 13.7 %copy-start.17 = (f32[128,128]{0,1:T(8,128)}, f32[128,128]{0,1:T(8,128)S(1)}, u32[]{:S(2)}) copy-start(f32[128,128]{0,1:T(8,128)S(1)} %fusion.123) | copy-start | bytes 196612
  30.8 0.8 copy-start.1
  33.7 1.0 copy-start.5
  37.3 4.8 %copy-start.6 = (f32[4,4,128,128]{2,3,1,0:T(8,128)S(1)}, f32[4,4,128,128]{2,3,1,0:T(8,128)}, u32[]{:S(2)}) copy-start(f32[4,4,128,128]{2,3,1,0:T(8,128)} %copy-done.5) | copy-start | bytes 3145732
  39.1 3.5 %copy-start.3 = (f32[4,4,64,128]{3,2,1,0:T(8,128)}, f32[4,4,64,128]{3,2,1,0:T(8,128)S(1)}, u32[]{:S(2)}) copy-start(f32[4,4,64,128]{3,2,1,0:T(8,128)S(1)} %fusion.53) | copy-start | bytes 1572868
  43.5 2.0 %copy-start.10 = (f32[4,128,128]{1,2,0:T(8,128)}, f32[4,128,128]{1,2,0:T(8,128)S(1)}, u32[]{:S(2)}) copy-start(f32[4,128,128]{1,2,0:T(8,128)S(1)} %get-tuple-element.149) | copy-start | bytes 786436
  44.8 1.5 copy-start.11
  44.8 3.9 %copy-start.24 = (f32[128]{0:T(128)S(1)}, f32[128]{0:T(128)}, u32[]{:S(2)}) copy-start(f32[128]{0:T(128)} %param.18) | copy-start | bytes 1540
  45.4 6.7 %copy-start.13 = (f32[4,1,128,128]{2,3,1,0:T(8,128)S(1)}, f32[4,1,128,128]{2,3,1,0:T(8,128)}, u32[]{:S(2)}) copy-start(f32[4,1,128,128]{2,3,1,0:T(8,128)} %get-tuple-element.129) | copy-start | bytes 786436
  55.3 1.7 copy-start.8
  55.3 1.7 copy-start.9
  55.3 3.8 %copy-start.12 = (f32[4,4,64,64]{3,2,1,0:T(8,128)S(1)}, f32[4,4,64,64]{3,2,1,0:T(8,128)}, u32[]{:S(2)}) copy-start(f32[4,4,64,64]{3,2,1,0:T(8,128)} %fusion.27) | copy-start | bytes 786436
  56.7 3.4 %copy-start.4 = (f32[4,4,64,128]{3,2,1,0:T(8,128)S(1)}, f32[4,4,64,128]{3,2,1,0:T(8,128)}, u32[]{:S(2)}) copy-start(f32[4,4,64,128]{3,2,1,0:T(8,128)} %copy-done.3) | copy-start | bytes 1572868
  57.0 3.7 %copy-start.2 = (f32[4,4,64,128]{3,2,1,0:T(8,128)S(1)}, f32[4,4,64,128]{3,2,1,0:T(8,128)}, u32[]{:S(2)}) copy-start(f32[4,4,64,128]{3,2,1,0:T(8,128)} %copy-done.1) | copy-start | bytes 1572868
  57.0 14.5 %collective-permute-start.4 = (bf16[4,128,256]{1,2,0:T(8,128)(2,1)S(1)}, bf16[4,128,256]{1,2,0:T(8,128)(2,1)S(1)}, u32[]{:S(2)}, u32[]{:S(2)}) collective-permute-start(bf16[4,128,256]{1,2,0:T(8,128)(2,1)S(1)} %pad_maximum_fusion.3), channel_id=1, source_target_pairs={{0,4},{4,8},{8,12},{12,16},{16,20},{20,24},{24,28},{28,32},{32,36}... | collective-permute-start | bytes 786440 | tf_op jit(solution)/shard_map/ppermute | solution.py:53
  60.7 2.8 %copy-start.7 = (f32[4,4,128,128]{2,3,1,0:T(8,128)S(1)}, f32[4,4,128,128]{2,3,1,0:T(8,128)}, u32[]{:S(2)}) copy-start(f32[4,4,128,128]{2,3,1,0:T(8,128)} %pad_maximum_fusion) | copy-start | bytes 3145732
  65.7 12.4 %copy-start.18 = (pred[256,256]{0,1:T(8,128)(4,1)S(1)}, pred[256,256]{0,1:T(8,128)(4,1)}, u32[]{:S(2)}) copy-start(pred[256,256]{0,1:T(8,128)(4,1)} %get-tuple-element.161) | copy-start | bytes 196612
  65.7 12.4 %copy-start.20 = (bf16[256,512]{1,0:T(8,128)(2,1)S(1)}, bf16[256,512]{1,0:T(8,128)(2,1)}, u32[]{:S(2)}) copy-start(bf16[256,512]{1,0:T(8,128)(2,1)} %param.20) | copy-start | bytes 786436
  72.0 6.7 %copy-start.14 = (bf16[256,512]{1,0:T(8,128)(2,1)S(1)}, bf16[256,512]{1,0:T(8,128)(2,1)}, u32[]{:S(2)}) copy-start(bf16[256,512]{1,0:T(8,128)(2,1)} %param.21) | copy-start | bytes 786436
  72.1 13.1 %collective-permute-start.5 = (bf16[4,128,256]{1,2,0:T(8,128)(2,1)S(1)}, bf16[4,128,256]{1,2,0:T(8,128)(2,1)S(1)}, u32[]{:S(2)}, u32[]{:S(2)}) collective-permute-start(bf16[4,128,256]{1,2,0:T(8,128)(2,1)S(1)} %pad_maximum_fusion.4), channel_id=1, source_target_pairs={{0,8},{4,12},{8,16},{12,20},{16,24},{20,28},{24,32},{28,36},{32,40... | collective-permute-start | bytes 786440 | tf_op jit(solution)/shard_map/ppermute | solution.py:53
  85.2 5.2 %copy-start.16 = (pred[256,256]{0,1:T(8,128)(4,1)S(1)}, pred[256,256]{0,1:T(8,128)(4,1)}, u32[]{:S(2)}) copy-start(pred[256,256]{0,1:T(8,128)(4,1)} %get-tuple-element.162) | copy-start | bytes 196612
  85.7 12.6 %collective-permute-start.6 = (bf16[4,128,256]{1,2,0:T(8,128)(2,1)S(1)}, bf16[4,128,256]{1,2,0:T(8,128)(2,1)S(1)}, u32[]{:S(2)}, u32[]{:S(2)}) collective-permute-start(bf16[4,128,256]{1,2,0:T(8,128)(2,1)S(1)} %pad_maximum_fusion.5), channel_id=1, source_target_pairs={{0,16},{4,20},{8,24},{12,28},{16,32},{20,36},{24,40},{28,44},{32,4... | collective-permute-start | bytes 786440 | tf_op jit(solution)/shard_map/ppermute | solution.py:53
  98.3 4.5 %copy-start.15 = (pred[256,256]{0,1:T(8,128)(4,1)S(1)}, pred[256,256]{0,1:T(8,128)(4,1)}, u32[]{:S(2)}) copy-start(pred[256,256]{0,1:T(8,128)(4,1)} %get-tuple-element.159) | copy-start | bytes 196612
  98.8 9.4 %collective-permute-start.7 = (bf16[4,128,256]{1,2,0:T(8,128)(2,1)S(1)}, bf16[4,128,256]{1,2,0:T(8,128)(2,1)S(1)}, u32[]{:S(2)}, u32[]{:S(2)}) collective-permute-start(bf16[4,128,256]{1,2,0:T(8,128)(2,1)S(1)} %pad_maximum_fusion.6), channel_id=1, source_target_pairs={{0,32},{4,36},{8,40},{12,44},{16,48},{20,52},{24,56},{28,60},{32,6... | collective-permute-start | bytes 786440 | tf_op jit(solution)/shard_map/ppermute | solution.py:53
  108.6 13.9 %collective-permute-start.8 = (bf16[4,128,256]{1,2,0:T(8,128)(2,1)S(1)}, bf16[4,128,256]{1,2,0:T(8,128)(2,1)S(1)}, u32[]{:S(2)}, u32[]{:S(2)}) collective-permute-start(bf16[4,128,256]{1,2,0:T(8,128)(2,1)S(1)} %pad_maximum_fusion.7), channel_id=1, source_target_pairs={{0,64},{4,68},{8,72},{12,76},{16,80},{20,84},{24,88},{28,92},{32,9... | collective-permute-start | bytes 786440 | tf_op jit(solution)/shard_map/ppermute | solution.py:53
  124.0 13.1 %collective-permute-start.9 = (bf16[4,128,128]{1,2,0:T(8,128)(2,1)S(1)}, bf16[4,128,128]{1,2,0:T(8,128)(2,1)S(1)}, u32[]{:S(2)}, u32[]{:S(2)}) collective-permute-start(bf16[4,128,128]{1,2,0:T(8,128)(2,1)S(1)} %get-tuple-element.109), channel_id=1, source_target_pairs={{0,128},{4,132},{8,136},{12,140},{16,144},{20,148},{24,152},{28,15... | collective-permute-start | bytes 393224 | tf_op jit(solution)/shard_map/ppermute | solution.py:53
  138.1 8.6 %collective-permute-start.10 = (bf16[4,128,128]{1,2,0:T(8,128)(2,1)}, bf16[4,128,128]{1,2,0:T(8,128)(2,1)S(1)}, u32[]{:S(2)}, u32[]{:S(2)}) collective-permute-start(bf16[4,128,128]{1,2,0:T(8,128)(2,1)} %fusion.7), channel_id=1, source_target_pairs={{0,4},{4,8},{8,12},{12,16},{16,20},{20,24},{24,28},{28,32},{32,36}... | collective-permute-start | bytes 393224 | tf_op jit(solution)/shard_map/ppermute | solution.py:53
  144.9 3.3 %copy-start.23 = (f32[512]{0:T(512)S(1)}, f32[512]{0:T(512)}, u32[]{:S(2)}) copy-start(f32[512]{0:T(512)} %broadcast_bitcast_fusion) | copy-start | bytes 6148
